TPU v7x, 1024 devices: a whole 8x8x8 slice. The times are simulated.
1024 devices in a mesh: band: 32 (over x_lo, z, core), pw: 32 (over x_hi, y).
Axes of the slice: x: 8 (x_hi: 4, x_lo: 2; x = x_hi * 2 + x_lo), y: 8, z: 8, core: 2. Of those that a mesh axis runs over, the one named last changes fastest.
Arguments:
- orbitals: float32 [2, 32, 110592], P(None, 'band', 'pw'), may hold values from -6 to 6
- pw_index: int32 [110592], P('pw'), may hold values from 0 to 27647, as said below
- potential: float32 [96, 96, 96], P(None, 'pw'), may hold values from -1 to 2
Outputs:
- applied: float32 [2, 32, 110592], P(None, 'band', 'pw')
- gram: float32 [2, 32, 32], P(None, 'band')
Inputs may be any that keep to these rules, and one draw needn't show every extreme that they name: `pw_index`: entry j of each device's block of 3456 entries names one of cells 8 j to 8 j + 7 of that device's 3 x 96 x 96 slab, counted with the last dimension fastest.
All inputs are finite; a program needn't handle non-finite values.
Results may differ from a plain program's by a relative error of at most 0.000053.
Values sent between devices are 32-bit elements; how exact they have to be, the bound alone decides.
No kernel may reach another device: no remote copies, remote signals or barrier semaphores. Data moves between devices by JAX's collectives and lax.ppermute only.
A program may use at most 32 MiB of HBM per device.

v0:
```python
import math

import jax
import jax.numpy as jnp
from jax import lax
from jax.sharding import PartitionSpec as P


def dft_tables(length):
    indices = lax.iota(jnp.int32, length)
    product = indices[:, None] * indices[None, :] % length
    angles = product.astype(jnp.float32) * (2.0 * math.pi / length)
    return (jnp.cos(angles), jnp.sin(angles))


def apply_dft(real_part, imag_part, form, cosine_table, sine_table, inverse):

    def contract(values, table):
        return jnp.einsum(form, values, table, precision=lax.Precision.HIGHEST)

    real_cos = contract(real_part, cosine_table)
    imag_sin = contract(imag_part, sine_table)
    real_sin = contract(real_part, sine_table)
    imag_cos = contract(imag_part, cosine_table)
    if inverse:
        return (real_cos - imag_sin, real_sin + imag_cos)
    return (real_cos + imag_sin, imag_cos - real_sin)


def pair_products(left, right):
    dims = (((1,), (1,)), ((), ()))
    highest = lax.Precision.HIGHEST
    first, second = (left[0], left[1])
    other_first, other_second = (right[0], right[1])
    gram_real = lax.dot_general(first, other_first, dims, precision=highest) + lax.dot_general(
        second, other_second, dims, precision=highest
    )
    gram_imag = lax.dot_general(first, other_second, dims, precision=highest) - lax.dot_general(
        second, other_first, dims, precision=highest
    )
    return jnp.stack([gram_real, gram_imag])


def local(orbitals, pw_index, potential):
    bands_here = orbitals.shape[1]
    columns = orbitals.shape[2]
    grid_size = potential.shape[0]
    planes = grid_size // lax.axis_size("pw")
    cosine_table, sine_table = dft_tables(grid_size)
    inv_cosine = cosine_table / grid_size
    inv_sine = sine_table / grid_size
    empty_slab = jnp.zeros((bands_here, planes * grid_size * grid_size), jnp.float32)
    slab_real = (
        empty_slab.at[:, pw_index]
        .set(orbitals[0])
        .reshape(bands_here, planes, grid_size, grid_size)
    )
    slab_imag = (
        empty_slab.at[:, pw_index]
        .set(orbitals[1])
        .reshape(bands_here, planes, grid_size, grid_size)
    )
    slab_real, slab_imag = apply_dft(
        slab_real, slab_imag, "bxyk,kn->bxyn", inv_cosine, inv_sine, True
    )
    slab_real, slab_imag = apply_dft(
        slab_real, slab_imag, "bxkz,kn->bxnz", inv_cosine, inv_sine, True
    )
    piece_real = lax.all_to_all(slab_real, "pw", split_axis=2, concat_axis=1, tiled=True)
    piece_imag = lax.all_to_all(slab_imag, "pw", split_axis=2, concat_axis=1, tiled=True)
    piece_real, piece_imag = apply_dft(
        piece_real, piece_imag, "bkyz,kn->bnyz", inv_cosine, inv_sine, True
    )
    piece_real = piece_real * potential[None]
    piece_imag = piece_imag * potential[None]
    piece_real, piece_imag = apply_dft(
        piece_real, piece_imag, "bkyz,kn->bnyz", cosine_table, sine_table, False
    )
    back_real = lax.all_to_all(piece_real, "pw", split_axis=1, concat_axis=2, tiled=True)
    back_imag = lax.all_to_all(piece_imag, "pw", split_axis=1, concat_axis=2, tiled=True)
    back_real, back_imag = apply_dft(
        back_real, back_imag, "bxkz,kn->bxnz", cosine_table, sine_table, False
    )
    back_real, back_imag = apply_dft(
        back_real, back_imag, "bxyk,kn->bxyn", cosine_table, sine_table, False
    )
    flat_real = back_real.reshape(bands_here, planes * grid_size * grid_size)
    flat_imag = back_imag.reshape(bands_here, planes * grid_size * grid_size)
    applied = jnp.stack([flat_real[:, pw_index], flat_imag[:, pw_index]])
    block = pair_products(orbitals, lax.all_gather(orbitals, "band", axis=1, tiled=True))
    total_pw = columns * lax.axis_size("pw")
    gram_matrix = lax.psum(block, "pw") / total_pw
    return (applied, gram_matrix)


def solution(mesh):
    placed = (P(None, "band", "pw"), P("pw"), P(None, "pw", None))
    return jax.shard_map(
        local,
        mesh=mesh,
        in_specs=placed,
        out_specs=(P(None, "band", "pw"), P(None, "band", None)),
        check_vma=False,
    )
```

profile of v0, /device:TPU:2, one launch (start us, length us, event | category | flops | bytes accessed | tf_op | source)
XLA Modules:
  0.0 283.8 jit_solution(2456923983475679707)
XLA Ops:
  0.6 0.7 compare_select_fusion
  1.4 17.1 %scatter_custom_fusion = f32[27648]{0:T(1024)S(1)} fusion(s32[3456]{0:T(1024)S(1)} %compare_select_fusion, f32[3456]{0:T(1024)S(1)} %get-tuple-element.3, f32[]{:T(128)} %constant.23.clone.1), kind=kCustom, calls=%fused_computation.43 | custom fusion | bytes 110596 | tf_op jit(solution)/shard_map/scatter | solution.py:55
  19.6 17.1 %scatter_custom_fusion.1 = f32[27648]{0:T(1024)S(1)} fusion(s32[3456]{0:T(1024)S(1)} %compare_select_fusion, f32[3456]{0:T(1024)S(1)} %get-tuple-element.2, f32[]{:T(128)} %constant.23.clone.1), kind=kCustom, calls=%fused_computation.41 | custom fusion | bytes 110596 | tf_op jit(solution)/shard_map/scatter | solution.py:60
  37.7 0.5 fusion.46
  38.2 0.5 fusion.5
  38.8 0.8 copy.76
  39.6 12.0 %all-to-all-start = ((f32[1,3,96,96]{3,0,1,2:T(1,128)}), f32[1,3,96,96]{3,0,1,2:T(1,128)S(1)}, u32[]{:S(2)}, u32[]{:S(2)}) async-start(f32[1,3,96,96]{3,0,1,2:T(1,128)} %copy.76), calls=%async_computation | async-start | bytes 294912 | tf_op jit(solution)/shard_map/all_to_all | solution.py:69
  52.1 0.5 fusion.4
  52.6 0.8 copy.82
  53.4 49.0 %all_gather.3 = f32[2,32,3456]{2,0,1:T(2,128)S(1)} all-gather(f32[2,1,3456]{2,0,1:T(2,128)S(1)} %copy.100), channel_id=1, replica_groups=mesh['band'=32,'pw'=32] {'band'}, dimensions={1}, use_global_device_ids=true | all-gather | bytes 912384 | tf_op jit(solution)/shard_map/all_gather | solution.py:90
  102.4 0.7 fusion.269
  105.0 83.1 %psum.7 = f32[2,1,32]{2,1,0:T(1,128)S(1)} all-reduce(f32[2,1,32]{2,1,0:T(1,128)S(1)} %pad_maximum_fusion.1), channel_id=1, replica_groups=mesh['band'=32,'pw'=32] {'pw'}, use_global_device_ids=true, to_apply=%region_2.3 | all-reduce | flops 64 | bytes 512 | tf_op jit(solution)/shard_map/psum | solution.py:92
  188.1 4.1 %all-to-all-start.1 = ((f32[1,3,96,96]{3,0,1,2:T(1,128)}), f32[1,3,96,96]{3,0,1,2:T(1,128)S(1)}, u32[]{:S(2)}, u32[]{:S(2)}) async-start(f32[1,3,96,96]{3,0,1,2:T(1,128)} %copy.82), calls=%async_computation.1 | async-start | bytes 294912 | tf_op jit(solution)/shard_map/all_to_all | solution.py:70
  193.5 11.1 %all-to-all-done.1 = f32[1,3,96,96]{3,0,1,2:T(1,128)S(1)} async-done(((f32[1,3,96,96]{3,0,1,2:T(1,128)}), f32[1,3,96,96]{3,0,1,2:T(1,128)S(1)}, u32[]{:S(2)}, u32[]{:S(2)}) %all-to-all-start.1) | async-done | bytes 110624 | tf_op jit(solution)/shard_map/all_to_all | solution.py:70
  205.0 0.8 copy-done
  205.8 0.5 fusion.7
  206.3 0.5 fusion.6
  207.4 0.5 fusion.2
  207.9 0.8 copy.95
  208.7 3.9 %all-to-all-start.3 = ((f32[1,96,3,96]{3,0,2,1:T(1,128)}), f32[1,96,3,96]{3,0,2,1:T(1,128)S(1)}, u32[]{:S(2)}, u32[]{:S(2)}) async-start(f32[1,96,3,96]{3,0,2,1:T(1,128)} %copy.95), calls=%async_computation.3 | async-start | bytes 294912 | tf_op jit(solution)/shard_map/all_to_all | solution.py:80
  213.1 0.5 fusion.3
  213.6 0.8 copy.90
  214.4 11.2 %all-to-all-done.3 = f32[1,96,3,96]{3,0,2,1:T(1,128)S(1)} async-done(((f32[1,96,3,96]{3,0,2,1:T(1,128)}), f32[1,96,3,96]{3,0,2,1:T(1,128)S(1)}, u32[]{:S(2)}, u32[]{:S(2)}) %all-to-all-start.3) | async-done | bytes 110624 | tf_op jit(solution)/shard_map/all_to_all | solution.py:80
  225.7 3.9 %all-to-all-start.2 = ((f32[1,96,3,96]{3,0,2,1:T(1,128)}), f32[1,96,3,96]{3,0,2,1:T(1,128)S(1)}, u32[]{:S(2)}, u32[]{:S(2)}) async-start(f32[1,96,3,96]{3,0,2,1:T(1,128)} %copy.90), calls=%async_computation.2 | async-start | bytes 294912 | tf_op jit(solution)/shard_map/all_to_all | solution.py:79
  229.6 0.6 broadcast_multiply_fusion
  230.2 11.9 %all-to-all-done.2 = f32[1,96,3,96]{3,0,2,1:T(1,128)S(1)} async-done(((f32[1,96,3,96]{3,0,2,1:T(1,128)}), f32[1,96,3,96]{3,0,2,1:T(1,128)S(1)}, u32[]{:S(2)}, u32[]{:S(2)}) %all-to-all-start.2) | async-done | bytes 110624 | tf_op jit(solution)/shard_map/all_to_all | solution.py:79
  242.3 0.5 fusion.60
  242.8 0.5 fusion.50
  243.9 0.5 fusion
  246.0 18.2 %gather_fusion.1 = f32[3456]{0:T(1024)S(1)} fusion(f32[27648]{0:T(1024)S(1)} %reshape.162, s32[4096]{0:T(1024)S(1)} %pad_clamp_fusion), kind=kCustom, calls=%fused_computation.1 | custom fusion | bytes 41472 | tf_op jit(solution)/shard_map/gather | solution.py:89
  264.9 18.2 %gather_fusion = f32[3456]{0:T(1024)S(1)} fusion(f32[27648]{0:T(1024)S(1)} %reshape.152, s32[4096]{0:T(1024)S(1)} %pad_clamp_fusion), kind=kCustom, calls=%fused_computation | custom fusion | bytes 41472 | tf_op jit(solution)/shard_map/gather | solution.py:89
  283.1 0.6 pad_maximum_fusion
  (42 shorter events, 10.1 us)
Async XLA Ops:
  0.6 0.7 copy-start.1
  39.6 148.5 %all-to-all-start = ((f32[1,3,96,96]{3,0,1,2:T(1,128)}), f32[1,3,96,96]{3,0,1,2:T(1,128)S(1)}, u32[]{:S(2)}, u32[]{:S(2)}) async-start(f32[1,3,96,96]{3,0,1,2:T(1,128)} %copy.76), calls=%async_computation | async-start | bytes 294912 | tf_op jit(solution)/shard_map/all_to_all | solution.py:69
  188.1 16.6 %all-to-all-start.1 = ((f32[1,3,96,96]{3,0,1,2:T(1,128)}), f32[1,3,96,96]{3,0,1,2:T(1,128)S(1)}, u32[]{:S(2)}, u32[]{:S(2)}) async-start(f32[1,3,96,96]{3,0,1,2:T(1,128)} %copy.82), calls=%async_computation.1 | async-start | bytes 294912 | tf_op jit(solution)/shard_map/all_to_all | solution.py:70
  204.9 0.9 copy-start
  208.7 17.0 %all-to-all-start.3 = ((f32[1,96,3,96]{3,0,2,1:T(1,128)}), f32[1,96,3,96]{3,0,2,1:T(1,128)S(1)}, u32[]{:S(2)}, u32[]{:S(2)}) async-start(f32[1,96,3,96]{3,0,2,1:T(1,128)} %copy.95), calls=%async_computation.3 | async-start | bytes 294912 | tf_op jit(solution)/shard_map/all_to_all | solution.py:80
  225.7 16.5 %all-to-all-start.2 = ((f32[1,96,3,96]{3,0,2,1:T(1,128)}), f32[1,96,3,96]{3,0,2,1:T(1,128)S(1)}, u32[]{:S(2)}, u32[]{:S(2)}) async-start(f32[1,96,3,96]{3,0,2,1:T(1,128)} %copy.90), calls=%async_computation.2 | async-start | bytes 294912 | tf_op jit(solution)/shard_map/all_to_all | solution.py:79
where the time goes:
time: 284 us
  blocking collectives  132 us (46%)
  local copies, waits for them, and re-layouts  76.7 us (27%)
  waiting for transfers between devices  34.3 us (12%)
  starting transfers between devices  23.8 us (8%)
  matrix products  14 us (5%)
    psum x1, blocking collectives, local(): gram_matrix = lax.psum(block, 'pw') / total_pw  83.1 us
    all_gather x1, blocking collectives, local(): lax.all_gather(orbitals, 'band', axis=1, tiled=True)  49 us
    gather x2, local copies, waits for them, and re-layouts, local(): applied = jnp.stack([flat_real[:, pw_index], flat_imag[:, pw_index]])  36.5 us
    scatter x1, local copies, waits for them, and re-layouts, local(): slab_real = empty_slab.at[:, pw_index].set(orbitals[0]).reshape(bands_her...  17.1 us
    scatter x1, local copies, waits for them, and re-layouts, local(): slab_imag = empty_slab.at[:, pw_index].set(orbitals[1]).reshape(bands_her...  17.1 us
    dot_general x24, matrix products, contract(): return jnp.einsum(form, values, table, precision=lax.Precision.HIGHEST)  12.1 us
    all_to_all x1, starting transfers between devices, local(): lax.all_to_all(slab_real, 'pw', split_axis=2, concat_axis=1, tiled=True)  12 us
    all_to_all x1, waiting for transfers between devices, local(): lax.all_to_all(piece_real, 'pw', split_axis=1, concat_axis=2, tiled=True)  11.9 us
  transfers between devices with their start and end apart: 4, of which 3 were waited for; matrix products, arithmetic and copies ran while one was open for 3% of the time, Pallas kernels for 0%

commit v1 on v0

v1 whole, which is shorter than its diff:
```python
import math

import jax
import jax.numpy as jnp
from jax import lax
from jax.sharding import PartitionSpec as P

HIGHEST = lax.Precision.HIGHEST


def dft_table(length, inverse, rows, cols):
    indices = lax.iota(jnp.int32, length)
    product = indices[:, None] * indices[None, :] % length
    angles = product.astype(jnp.float32) * (2.0 * math.pi / length)
    cos, sin = jnp.cos(angles), jnp.sin(angles)
    if inverse:
        cos, sin = cos / length, sin / length
        table = jnp.stack([jnp.stack([cos, sin], 1), jnp.stack([-sin, cos], 1)], 0)
    else:
        table = jnp.stack([jnp.stack([cos, -sin], 1), jnp.stack([sin, cos], 1)], 0)
    perm_in = (0, 1) if rows == "ck" else (1, 0)
    perm_out = (2, 3) if cols == "dn" else (3, 2)
    table = jnp.transpose(table, perm_in + perm_out)
    return table.reshape(2 * length, 2 * length)


def contract(values, table, form):
    return jnp.einsum(form, values, table, precision=HIGHEST)


def gram_rows(orbitals):
    _, bands_here, columns = orbitals.shape
    n_band = lax.axis_size("band")
    n_pw = lax.axis_size("pw")
    chunk = columns // n_band
    pieces = orbitals.reshape(2, bands_here, n_band, chunk)
    pieces = lax.all_to_all(pieces, "band", split_axis=2, concat_axis=1, tiled=True)
    bands = bands_here * n_band
    stacked = pieces.reshape(2 * bands, chunk)
    prod = lax.dot_general(stacked, stacked, (((1,), (1,)), ((), ())), precision=HIGHEST)
    gram_real = prod[:bands, :bands] + prod[bands:, bands:]
    gram_imag = prod[:bands, bands:] - prod[bands:, :bands]
    partial = jnp.stack([gram_real, gram_imag]).reshape(1, 2, n_band, bands_here, bands)
    rows = lax.all_to_all(partial, "band", split_axis=2, concat_axis=0, tiled=True)
    rows = jnp.sum(rows, axis=0).reshape(1, 2, bands_here, bands)
    spread = jnp.broadcast_to(rows, (n_pw, 2, bands_here, bands))
    spread = lax.all_to_all(spread, "pw", split_axis=0, concat_axis=0, tiled=True)
    total = jnp.sum(spread, axis=0)
    return total / (columns * n_pw)


def local(orbitals, pw_index, potential):
    _, bands_here, columns = orbitals.shape
    grid = potential.shape[0]
    planes = potential.shape[1]
    blocks = grid // 8
    offsets = (pw_index - 8 * lax.iota(jnp.int32, columns)).reshape(planes, grid, blocks)
    lanes = lax.iota(jnp.int32, 8)
    hit = offsets[..., None] == lanes

    coeffs = orbitals.reshape(2, bands_here, planes, grid, blocks)
    coeffs = jnp.transpose(coeffs, (1, 2, 3, 0, 4))
    spread = jnp.where(hit[None, :, :, None], coeffs[..., None], 0.0)
    spread = spread.reshape(bands_here, planes, grid, 2 * grid)

    slab = contract(spread, dft_table(grid, True, "ck", "dn"), "bxyw,wv->bxyv")
    slab = slab.reshape(bands_here, planes, 2 * grid, grid)
    slab = contract(slab, dft_table(grid, True, "kc", "dn"), "bxwz,wv->bxvz")
    slab = slab.reshape(bands_here, planes, 2, grid, grid)
    piece = lax.all_to_all(slab, "pw", split_axis=3, concat_axis=1, tiled=True)
    piece = piece.reshape(bands_here, 2 * grid, planes, grid)
    piece = contract(piece, dft_table(grid, True, "kc", "nd"), "bwyz,wv->bvyz")
    piece = piece.reshape(bands_here, grid, 2, planes, grid) * potential[None, :, None]
    piece = piece.reshape(bands_here, 2 * grid, planes, grid)
    piece = contract(piece, dft_table(grid, False, "kc", "nd"), "bwyz,wv->bvyz")
    piece = piece.reshape(bands_here, grid, 2, planes, grid)
    back = lax.all_to_all(piece, "pw", split_axis=1, concat_axis=3, tiled=True)
    back = back.reshape(bands_here, planes, 2 * grid, grid)
    back = contract(back, dft_table(grid, False, "ck", "nd"), "bxwz,wv->bxvz")
    back = back.reshape(bands_here, planes, grid, 2 * grid)
    back = contract(back, dft_table(grid, False, "ck", "dn"), "bxyw,wv->bxyv")
    back = back.reshape(bands_here, planes, grid, 2, blocks, 8)
    picked = jnp.sum(jnp.where(hit[None, :, :, None], back, 0.0), axis=-1)
    applied = jnp.transpose(picked, (3, 0, 1, 2, 4)).reshape(2, bands_here, columns)
    return (applied, gram_rows(orbitals))


def solution(mesh):
    placed = (P(None, "band", "pw"), P("pw"), P(None, "pw", None))
    return jax.shard_map(
        local,
        mesh=mesh,
        in_specs=placed,
        out_specs=(P(None, "band", "pw"), P(None, "band", None)),
        check_vma=False,
    )
```

time: 284 us -> 120 us (0.42)
  the two profiles are of different devices: /device:TPU:2 before, /device:TPU:16 now
where the time goes in v1:
time: 120 us; the launch traced here: 119 us
  starting transfers between devices  49.2 us (41%)
  local copies, waits for them, and re-layouts  34 us (28%)
  waiting for transfers between devices  28.2 us (24%)
  matrix products  3.66 us (3%)
  other arithmetic  3.39 us (3%)
    all_to_all x1, starting transfers between devices, gram_rows(): lax.all_to_all(pieces, 'band', split_axis=2, concat_axis=1, tiled=True)  18 us
    reshape x6, local copies, waits for them, and re-layouts, dft_table(): return table.reshape(2 * length, 2 * length)  16.1 us
    all_to_all x1, waiting for transfers between devices, local(): back = lax.all_to_all(piece, 'pw', split_axis=1, concat_axis=3, tiled=True)  12.8 us
    all_to_all x1, starting transfers between devices, local(): piece = lax.all_to_all(slab, 'pw', split_axis=3, concat_axis=1, tiled=True)  12.1 us
    transpose x4, local copies, waits for them, and re-layouts, dft_table(): table = jnp.transpose(table, perm_in + perm_out)  10.4 us
    all_to_all x1, starting transfers between devices, gram_rows(): lax.all_to_all(spread, 'pw', split_axis=0, concat_axis=0, tiled=True)  10.3 us
    all_to_all x1, waiting for transfers between devices, gram_rows(): lax.all_to_all(spread, 'pw', split_axis=0, concat_axis=0, tiled=True)  8.78 us
    all_to_all x1, starting transfers between devices, local(): back = lax.all_to_all(piece, 'pw', split_axis=1, concat_axis=3, tiled=True)  5.05 us
  transfers between devices with their start and end apart: 5, of which 4 were waited for; matrix products, arithmetic and copies ran while one was open for 30% of the time, Pallas kernels for 0%

profile of v1, /device:TPU:16, one launch (start us, length us, event | category | flops | bytes accessed | tf_op | source)
XLA Modules:
  0.0 119.4 jit_solution(6862877449002950498)
XLA Ops:
  0.6 0.8 reduce.7
  1.6 0.6 copy.225
  2.2 18.0 %all-to-all-start.2 = ((f32[2,1,32,108]{3,0,1,2:T(2,128)}), f32[2,1,32,108]{3,0,1,2:T(2,128)S(1)}, u32[]{:S(2)}, u32[]{:S(2)}) async-start(f32[2,1,32,108]{3,0,1,2:T(2,128)} %copy.225), calls=%async_computation.2 | async-start | bytes 65536 | tf_op jit(solution)/shard_map/all_to_all | solution.py:37
  20.2 0.2 broadcast_multiply_fusion
  20.7 0.3 reshape.232
  21.5 0.7 multiply_subtract_fusion
  22.7 0.7 fusion.23
  23.9 4.8 %all-to-all-done.2 = f32[2,1,32,108]{3,0,1,2:T(2,128)S(1)} async-done(((f32[2,1,32,108]{3,0,1,2:T(2,128)}), f32[2,1,32,108]{3,0,1,2:T(2,128)S(1)}, u32[]{:S(2)}, u32[]{:S(2)}) %all-to-all-start.2) | async-done | bytes 27680 | tf_op jit(solution)/shard_map/all_to_all | solution.py:37
  28.9 0.6 copy.227
  29.6 3.8 %all-to-all-start.3 = ((f32[1,2,32,1,32]{4,1,3,0,2:T(2,128)}), f32[1,2,32,1,32]{4,1,3,0,2:T(2,128)S(1)}, u32[]{:S(2)}, u32[]{:S(2)}) async-start(f32[1,2,32,1,32]{4,1,3,0,2:T(2,128)} %copy.227), calls=%async_computation.3 | async-start | bytes 65536 | tf_op jit(solution)/shard_map/all_to_all | solution.py:44
  33.4 0.7 fusion.4
  34.1 0.9 copy.213
  35.0 5.0 %copy.205 = f32[96,2,96,2]{3,2,1,0:T(8,128)} copy(f32[96,2,96,2]{2,0,3,1:T(8,128)S(1)} %get-tuple-element.23) | data formatting | bytes 294912 | tf_op jit(solution)/shard_map/transpose | solution.py:23
  40.0 7.7 %reshape.230 = f32[192,192]{1,0:T(8,128)S(1)} reshape(f32[96,2,96,2]{3,2,1,0:T(8,128)} %copy.205) | data formatting | bytes 294912 | tf_op jit(solution)/shard_map/reshape | solution.py:24
  48.0 12.1 %all-to-all-start = ((f32[1,3,2,96,96]{4,2,1,0,3:T(2,128)}), f32[1,3,2,96,96]{4,2,1,0,3:T(2,128)S(1)}, u32[]{:S(2)}, u32[]{:S(2)}) async-start(f32[1,3,2,96,96]{4,2,1,0,3:T(2,128)} %copy.213), calls=%async_computation | async-start | bytes 589824 | tf_op jit(solution)/shard_map/all_to_all | solution.py:70
  60.3 0.2 fusion.12
  60.6 5.1 %copy.203 = f32[96,2,96,2]{3,2,1,0:T(8,128)} copy(f32[96,2,96,2]{2,0,3,1:T(8,128)S(1)} %get-tuple-element.22) | data formatting | bytes 294912 | tf_op jit(solution)/shard_map/transpose | solution.py:23
  65.7 7.7 %reshape.228 = f32[192,192]{1,0:T(8,128)S(1)} reshape(f32[96,2,96,2]{3,2,1,0:T(8,128)} %copy.203) | data formatting | bytes 294912 | tf_op jit(solution)/shard_map/reshape | solution.py:24
  73.7 1.9 %all-to-all-done = f32[1,3,2,96,96]{4,2,1,0,3:T(2,128)S(1)} async-done(((f32[1,3,2,96,96]{4,2,1,0,3:T(2,128)}), f32[1,3,2,96,96]{4,2,1,0,3:T(2,128)S(1)}, u32[]{:S(2)}, u32[]{:S(2)}) %all-to-all-start) | async-done | bytes 221216 | tf_op jit(solution)/shard_map/all_to_all | solution.py:70
  75.6 0.6 broadcast_in_dim.32
  76.2 10.3 %all-to-all-start.4 = ((f32[32,2,1,32]{3,2,1,0:T(1,128)}), f32[32,2,1,32]{3,2,1,0:T(1,128)S(1)}, u32[]{:S(2)}, u32[]{:S(2)}) async-start(f32[32,2,1,32]{3,2,1,0:T(1,128)} %broadcast_in_dim.32), calls=%async_computation.4 | async-start | bytes 65536 | tf_op jit(solution)/shard_map/all_to_all | solution.py:47
  86.8 0.5 convolution_multiply_fusion
  87.3 0.2 copy.217
  87.5 0.5 convolution_bitcast_fusion.1
  88.0 0.9 copy.219
  88.9 8.8 %all-to-all-done.4 = f32[32,2,1,32]{3,2,1,0:T(1,128)S(1)} async-done(((f32[32,2,1,32]{3,2,1,0:T(1,128)}), f32[32,2,1,32]{3,2,1,0:T(1,128)S(1)}, u32[]{:S(2)}, u32[]{:S(2)}) %all-to-all-start.4) | async-done | bytes 8224 | tf_op jit(solution)/shard_map/all_to_all | solution.py:47
  97.7 5.1 %all-to-all-start.1 = ((f32[1,96,2,3,96]{4,2,3,0,1:T(2,128)}), f32[1,96,2,3,96]{4,2,3,0,1:T(2,128)S(1)}, u32[]{:S(2)}, u32[]{:S(2)}) async-start(f32[1,96,2,3,96]{4,2,3,0,1:T(2,128)} %copy.219), calls=%async_computation.1 | async-start | bytes 589824 | tf_op jit(solution)/shard_map/all_to_all | solution.py:77
  103.6 0.6 broadcast_multiply_fusion.2
  104.2 12.8 %all-to-all-done.1 = f32[1,96,2,3,96]{4,2,3,0,1:T(2,128)S(1)} async-done(((f32[1,96,2,3,96]{4,2,3,0,1:T(2,128)}), f32[1,96,2,3,96]{4,2,3,0,1:T(2,128)S(1)}, u32[]{:S(2)}, u32[]{:S(2)}) %all-to-all-start.1) | async-done | bytes 221216 | tf_op jit(solution)/shard_map/all_to_all | solution.py:77
  117.2 0.5 convolution_bitcast_fusion
  117.8 0.6 fusion
  118.6 0.9 reshape.257
  (42 shorter events, 4.2 us)
Async XLA Ops:
  2.2 26.4 %all-to-all-start.2 = ((f32[2,1,32,108]{3,0,1,2:T(2,128)}), f32[2,1,32,108]{3,0,1,2:T(2,128)S(1)}, u32[]{:S(2)}, u32[]{:S(2)}) async-start(f32[2,1,32,108]{3,0,1,2:T(2,128)} %copy.225), calls=%async_computation.2 | async-start | bytes 65536 | tf_op jit(solution)/shard_map/all_to_all | solution.py:37
  29.6 18.4 %all-to-all-start.3 = ((f32[1,2,32,1,32]{4,1,3,0,2:T(2,128)}), f32[1,2,32,1,32]{4,1,3,0,2:T(2,128)S(1)}, u32[]{:S(2)}, u32[]{:S(2)}) async-start(f32[1,2,32,1,32]{4,1,3,0,2:T(2,128)} %copy.227), calls=%async_computation.3 | async-start | bytes 65536 | tf_op jit(solution)/shard_map/all_to_all | solution.py:44
  48.0 27.6 %all-to-all-start = ((f32[1,3,2,96,96]{4,2,1,0,3:T(2,128)}), f32[1,3,2,96,96]{4,2,1,0,3:T(2,128)S(1)}, u32[]{:S(2)}, u32[]{:S(2)}) async-start(f32[1,3,2,96,96]{4,2,1,0,3:T(2,128)} %copy.213), calls=%async_computation | async-start | bytes 589824 | tf_op jit(solution)/shard_map/all_to_all | solution.py:70
  60.6 26.2 %copy-start = (f32[96,3,96]{2,0,1:T(8,128)S(1)}, f32[96,3,96]{2,0,1:T(8,128)}, u32[]{:S(2)}) copy-start(f32[96,3,96]{2,0,1:T(8,128)} %param.5) | copy-start | bytes 331780
  76.2 21.5 %all-to-all-start.4 = ((f32[32,2,1,32]{3,2,1,0:T(1,128)}), f32[32,2,1,32]{3,2,1,0:T(1,128)S(1)}, u32[]{:S(2)}, u32[]{:S(2)}) async-start(f32[32,2,1,32]{3,2,1,0:T(1,128)} %broadcast_in_dim.32), calls=%async_computation.4 | async-start | bytes 65536 | tf_op jit(solution)/shard_map/all_to_all | solution.py:47
  97.7 19.2 %all-to-all-start.1 = ((f32[1,96,2,3,96]{4,2,3,0,1:T(2,128)}), f32[1,96,2,3,96]{4,2,3,0,1:T(2,128)S(1)}, u32[]{:S(2)}, u32[]{:S(2)}) async-start(f32[1,96,2,3,96]{4,2,3,0,1:T(2,128)} %copy.219), calls=%async_computation.1 | async-start | bytes 589824 | tf_op jit(solution)/shard_map/all_to_all | solution.py:77

commit v2 on v1

--- a/solution.py
+++ b/solution.py
@@ -1,6 +1,7 @@
 import math
 
 import jax
+import numpy as np
 import jax.numpy as jnp
 from jax import lax
 from jax.sharding import PartitionSpec as P
@@ -9,19 +10,18 @@
 
 
 def dft_table(length, inverse, rows, cols):
-    indices = lax.iota(jnp.int32, length)
-    product = indices[:, None] * indices[None, :] % length
-    angles = product.astype(jnp.float32) * (2.0 * math.pi / length)
-    cos, sin = jnp.cos(angles), jnp.sin(angles)
+    indices = np.arange(length)
+    angles = (np.outer(indices, indices) % length) * (2.0 * np.pi / length)
+    cos, sin = np.cos(angles), np.sin(angles)
     if inverse:
         cos, sin = cos / length, sin / length
-        table = jnp.stack([jnp.stack([cos, sin], 1), jnp.stack([-sin, cos], 1)], 0)
+        table = np.stack([np.stack([cos, sin], 1), np.stack([-sin, cos], 1)], 0)
     else:
-        table = jnp.stack([jnp.stack([cos, -sin], 1), jnp.stack([sin, cos], 1)], 0)
+        table = np.stack([np.stack([cos, -sin], 1), np.stack([sin, cos], 1)], 0)
     perm_in = (0, 1) if rows == "ck" else (1, 0)
     perm_out = (2, 3) if cols == "dn" else (3, 2)
-    table = jnp.transpose(table, perm_in + perm_out)
-    return table.reshape(2 * length, 2 * length)
+    table = np.transpose(table, perm_in + perm_out)
+    return jnp.asarray(table.reshape(2 * length, 2 * length).astype(np.float32))
 
 
 def contract(values, table, form):
@@ -31,7 +31,6 @@
 def gram_rows(orbitals):
     _, bands_here, columns = orbitals.shape
     n_band = lax.axis_size("band")
-    n_pw = lax.axis_size("pw")
     chunk = columns // n_band
     pieces = orbitals.reshape(2, bands_here, n_band, chunk)
     pieces = lax.all_to_all(pieces, "band", split_axis=2, concat_axis=1, tiled=True)
@@ -42,11 +41,7 @@
     gram_imag = prod[:bands, bands:] - prod[bands:, :bands]
     partial = jnp.stack([gram_real, gram_imag]).reshape(1, 2, n_band, bands_here, bands)
     rows = lax.all_to_all(partial, "band", split_axis=2, concat_axis=0, tiled=True)
-    rows = jnp.sum(rows, axis=0).reshape(1, 2, bands_here, bands)
-    spread = jnp.broadcast_to(rows, (n_pw, 2, bands_here, bands))
-    spread = lax.all_to_all(spread, "pw", split_axis=0, concat_axis=0, tiled=True)
-    total = jnp.sum(spread, axis=0)
-    return total / (columns * n_pw)
+    return jnp.sum(rows, axis=0).reshape(2, bands_here, bands)
 
 
 def local(orbitals, pw_index, potential):
@@ -57,6 +52,7 @@
     offsets = (pw_index - 8 * lax.iota(jnp.int32, columns)).reshape(planes, grid, blocks)
     lanes = lax.iota(jnp.int32, 8)
     hit = offsets[..., None] == lanes
+    rows = gram_rows(orbitals)
 
     coeffs = orbitals.reshape(2, bands_here, planes, grid, blocks)
     coeffs = jnp.transpose(coeffs, (1, 2, 3, 0, 4))
@@ -73,8 +69,17 @@
     piece = piece.reshape(bands_here, grid, 2, planes, grid) * potential[None, :, None]
     piece = piece.reshape(bands_here, 2 * grid, planes, grid)
     piece = contract(piece, dft_table(grid, False, "kc", "nd"), "bwyz,wv->bvyz")
-    piece = piece.reshape(bands_here, grid, 2, planes, grid)
-    back = lax.all_to_all(piece, "pw", split_axis=1, concat_axis=3, tiled=True)
+    n_pw = lax.axis_size("pw")
+    width = planes * 2 * planes * grid
+    payload = piece.reshape(bands_here, n_pw, width).transpose(1, 0, 2)
+    payload = payload.reshape(n_pw, bands_here * width)
+    extra = jnp.broadcast_to(rows.reshape(1, -1), (n_pw, rows.size))
+    payload = jnp.concatenate([payload, extra], axis=1)
+    payload = lax.all_to_all(payload, "pw", split_axis=0, concat_axis=0, tiled=True)
+    gram = jnp.sum(payload[:, bands_here * width :], axis=0).reshape(rows.shape)
+    gram = gram / (columns * n_pw)
+    back = payload[:, : bands_here * width].reshape(n_pw, bands_here, planes, 2, planes, grid)
+    back = jnp.transpose(back, (1, 2, 3, 0, 4, 5))
     back = back.reshape(bands_here, planes, 2 * grid, grid)
     back = contract(back, dft_table(grid, False, "ck", "nd"), "bxwz,wv->bxvz")
     back = back.reshape(bands_here, planes, grid, 2 * grid)
@@ -82,7 +87,7 @@
     back = back.reshape(bands_here, planes, grid, 2, blocks, 8)
     picked = jnp.sum(jnp.where(hit[None, :, :, None], back, 0.0), axis=-1)
     applied = jnp.transpose(picked, (3, 0, 1, 2, 4)).reshape(2, bands_here, columns)
-    return (applied, gram_rows(orbitals))
+    return (applied, gram)
 
 
 def solution(mesh):

time: 120 us -> 95.9 us (0.80)
  local copies, waits for them, and re-layouts: 34 us -> 11 us
  blocking collectives: 0 us -> 18 us
  starting transfers between devices: 49.2 us -> 33.9 us
  other arithmetic: 3.39 us -> 1.17 us
  waiting for transfers between devices: 28.2 us -> 26.9 us
    all_to_all x2 -> x0, waiting for transfers between devices: 21.5 us -> none  [the longest x1 12.8 us: local(): back = lax.all_to_all(piece, 'pw', split_axis=1, concat_axis=3, tiled=True)]
    all_to_all x0 -> x1, blocking collectives: none -> 18 us  [local(): lax.all_to_all(payload, 'pw', split_axis=0, concat_axis=0, tiled=True)]
    reshape x6 -> x1, local copies, waits for them, and re-layouts: 16.1 us -> 0.31 us  [local(): payload[:, :bands_here * width]]
    all_to_all x2 -> x0, starting transfers between devices: 15.4 us -> none  [the longest x1 10.3 us: gram_rows(): lax.all_to_all(spread, 'pw', split_axis=0, concat_axis=0, tiled=True)]
    all_to_all x1, waiting for transfers between devices: 1.89 us -> 14.5 us  [local(): piece = lax.all_to_all(slab, 'pw', split_axis=3, concat_axis=1, tiled=True)]
    transpose x4 -> x2, local copies, waits for them, and re-layouts: 10.4 us -> 0.28 us  [the longest x1 0.21 us: local(): payload = payload.reshape(n_pw, bands_here * width)]
    all_to_all x1, waiting for transfers between devices: 0.01 us -> 7 us  [gram_rows(): lax.all_to_all(partial, 'band', split_axis=2, concat_axis=0, tiled=True)]
    unnamed x2 -> x17, local copies, waits for them, and re-layouts: 0.01 us -> 4.39 us
  transfers between devices with their start and end apart: 5 -> 3, of which waited for: 4 -> 3; matrix products, arithmetic and copies ran while one was open for 30% -> 4% of each run, Pallas kernels for 0% -> 0%
where the time goes in v2:
time: 95.9 us; the launch traced here: 95.3 us
  starting transfers between devices  33.9 us (35%)
  waiting for transfers between devices  26.9 us (28%)
  blocking collectives  18 us (19%)
  local copies, waits for them, and re-layouts  11 us (11%)
  matrix products  3.44 us (4%)
  other arithmetic  1.17 us (1%)
    all_to_all x1, starting transfers between devices, gram_rows(): lax.all_to_all(pieces, 'band', split_axis=2, concat_axis=1, tiled=True)  18 us
    all_to_all x1, blocking collectives, local(): lax.all_to_all(payload, 'pw', split_axis=0, concat_axis=0, tiled=True)  18 us
    all_to_all x1, waiting for transfers between devices, local(): piece = lax.all_to_all(slab, 'pw', split_axis=3, concat_axis=1, tiled=True)  14.5 us
    all_to_all x1, starting transfers between devices, local(): piece = lax.all_to_all(slab, 'pw', split_axis=3, concat_axis=1, tiled=True)  12.1 us
    all_to_all x1, waiting for transfers between devices, gram_rows(): lax.all_to_all(partial, 'band', split_axis=2, concat_axis=0, tiled=True)  7 us
    all_to_all x1, waiting for transfers between devices, gram_rows(): lax.all_to_all(pieces, 'band', split_axis=2, concat_axis=1, tiled=True)  5.43 us
    unnamed x17, local copies, waits for them, and re-layouts  4.39 us
    all_to_all x1, starting transfers between devices, gram_rows(): lax.all_to_all(partial, 'band', split_axis=2, concat_axis=0, tiled=True)  3.8 us
  transfers between devices with their start and end apart: 3, of which 3 were waited for; matrix products, arithmetic and copies ran while one was open for 4% of the time, Pallas kernels for 0%

profile of v2, /device:TPU:16, one launch (start us, length us, event | category | flops | bytes accessed | tf_op | source)
XLA Modules:
  0.0 95.3 jit_solution(9538427021917824475)
XLA Ops:
  0.6 0.8 reduce.6
  1.6 0.6 copy.47
  2.2 18.0 %all-to-all-start.1 = ((f32[2,1,32,108]{3,0,1,2:T(2,128)}), f32[2,1,32,108]{3,0,1,2:T(2,128)S(1)}, u32[]{:S(2)}, u32[]{:S(2)}) async-start(f32[2,1,32,108]{3,0,1,2:T(2,128)} %copy.47), calls=%async_computation.1 | async-start | bytes 65536 | tf_op jit(solution)/shard_map/all_to_all | solution.py:36
  20.2 0.3 reshape.115
  20.6 0.4 copy-done.7
  21.5 0.8 copy-done.5
  22.4 0.7 fusion.6
  23.2 5.4 %all-to-all-done.1 = f32[2,1,32,108]{3,0,1,2:T(2,128)S(1)} async-done(((f32[2,1,32,108]{3,0,1,2:T(2,128)}), f32[2,1,32,108]{3,0,1,2:T(2,128)S(1)}, u32[]{:S(2)}, u32[]{:S(2)}) %all-to-all-start.1) | async-done | bytes 27680 | tf_op jit(solution)/shard_map/all_to_all | solution.py:36
  28.7 0.2 fusion.9
  28.9 0.6 copy.49
  29.6 3.8 %all-to-all-start.2 = ((f32[1,2,32,1,32]{4,1,3,0,2:T(2,128)}), f32[1,2,32,1,32]{4,1,3,0,2:T(2,128)S(1)}, u32[]{:S(2)}, u32[]{:S(2)}) async-start(f32[1,2,32,1,32]{4,1,3,0,2:T(2,128)} %copy.49), calls=%async_computation.2 | async-start | bytes 65536 | tf_op jit(solution)/shard_map/all_to_all | solution.py:43
  33.4 0.5 fusion.7
  33.9 0.9 copy.42
  34.8 7.0 %all-to-all-done.2 = f32[1,2,32,1,32]{4,1,3,0,2:T(2,128)S(1)} async-done(((f32[1,2,32,1,32]{4,1,3,0,2:T(2,128)}), f32[1,2,32,1,32]{4,1,3,0,2:T(2,128)S(1)}, u32[]{:S(2)}, u32[]{:S(2)}) %all-to-all-start.2) | async-done | bytes 8224 | tf_op jit(solution)/shard_map/all_to_all | solution.py:43
  41.8 12.1 %all-to-all-start = ((f32[1,3,2,96,96]{4,2,1,0,3:T(2,128)}), f32[1,3,2,96,96]{4,2,1,0,3:T(2,128)S(1)}, u32[]{:S(2)}, u32[]{:S(2)}) async-start(f32[1,3,2,96,96]{4,2,1,0,3:T(2,128)} %copy.42), calls=%async_computation | async-start | bytes 589824 | tf_op jit(solution)/shard_map/all_to_all | solution.py:66
  54.1 14.5 %all-to-all-done = f32[1,3,2,96,96]{4,2,1,0,3:T(2,128)S(1)} async-done(((f32[1,3,2,96,96]{4,2,1,0,3:T(2,128)}), f32[1,3,2,96,96]{4,2,1,0,3:T(2,128)S(1)}, u32[]{:S(2)}, u32[]{:S(2)}) %all-to-all-start) | async-done | bytes 221216 | tf_op jit(solution)/shard_map/all_to_all | solution.py:66
  68.8 0.8 copy-done.1
  69.6 0.5 convolution_multiply_fusion
  70.1 0.2 copy.45
  70.4 0.7 copy-done.3
  71.0 0.5 fusion.8
  71.5 0.2 copy.46
  71.7 0.2 transpose.33
  72.0 0.2 copy.50
  72.2 18.0 %all_to_all.45 = f32[32,1,1792]{2,1,0:T(1,128)S(1)} all-to-all(f32[32,1,1792]{2,1,0:T(1,128)S(1)} %copy.50), channel_id=1, replica_groups=mesh['band'=32,'pw'=32] {'pw'}, dimensions={0} | all-to-all | bytes 458752 | tf_op jit(solution)/shard_map/all_to_all | solution.py:78
  90.3 0.6 div.10
  90.9 0.3 reshape.123
  91.5 0.8 copy-done.2
  92.3 0.5 convolution_bitcast_fusion
  92.9 0.8 copy-done
  93.7 0.6 fusion
  94.5 0.9 reshape.140
  (35 shorter events, 1.9 us)
Async XLA Ops:
  2.2 26.4 %all-to-all-start.1 = ((f32[2,1,32,108]{3,0,1,2:T(2,128)}), f32[2,1,32,108]{3,0,1,2:T(2,128)S(1)}, u32[]{:S(2)}, u32[]{:S(2)}) async-start(f32[2,1,32,108]{3,0,1,2:T(2,128)} %copy.47), calls=%async_computation.1 | async-start | bytes 65536 | tf_op jit(solution)/shard_map/all_to_all | solution.py:36
  20.2 0.7 copy-start.7
  21.4 0.9 copy-start.5
  28.7 4.7 %copy-start.4 = (f32[192,192,1]{0,1,2:T(8,128)S(1)}, f32[192,192,1]{0,1,2:T(8,128)}, u32[]{:S(2)}) copy-start(f32[192,192,1]{0,1,2:T(8,128)} %constant.37) | copy-start | bytes 442372
  29.6 12.3 %all-to-all-start.2 = ((f32[1,2,32,1,32]{4,1,3,0,2:T(2,128)}), f32[1,2,32,1,32]{4,1,3,0,2:T(2,128)S(1)}, u32[]{:S(2)}, u32[]{:S(2)}) async-start(f32[1,2,32,1,32]{4,1,3,0,2:T(2,128)} %copy.49), calls=%async_computation.2 | async-start | bytes 65536 | tf_op jit(solution)/shard_map/all_to_all | solution.py:43
  41.8 26.8 %all-to-all-start = ((f32[1,3,2,96,96]{4,2,1,0,3:T(2,128)}), f32[1,3,2,96,96]{4,2,1,0,3:T(2,128)S(1)}, u32[]{:S(2)}, u32[]{:S(2)}) async-start(f32[1,3,2,96,96]{4,2,1,0,3:T(2,128)} %copy.42), calls=%async_computation | async-start | bytes 589824 | tf_op jit(solution)/shard_map/all_to_all | solution.py:66
  68.6 0.9 copy-start.1
  68.6 1.0 %copy-start.6 = (f32[96,3,96]{2,0,1:T(8,128)S(1)}, f32[96,3,96]{2,0,1:T(8,128)}, u32[]{:S(2)}) copy-start(f32[96,3,96]{2,0,1:T(8,128)} %param.11) | copy-start | bytes 331780
  70.1 0.9 copy-start.3
  91.3 0.9 copy-start.2
  92.8 1.0 %copy-start = (f32[2,12,8,192,1]{3,1,2,0,4:T(8,128)S(1)}, f32[2,12,8,192,1]{3,1,2,0,4:T(8,128)}, u32[]{:S(2)}) copy-start(f32[2,12,8,192,1]{3,1,2,0,4:T(8,128)} %constant.39) | copy-start | bytes 442372

commit v3 on v2

--- a/solution.py
+++ b/solution.py
@@ -31,17 +31,20 @@
 def gram_rows(orbitals):
     _, bands_here, columns = orbitals.shape
     n_band = lax.axis_size("band")
-    chunk = columns // n_band
-    pieces = orbitals.reshape(2, bands_here, n_band, chunk)
-    pieces = lax.all_to_all(pieces, "band", split_axis=2, concat_axis=1, tiled=True)
-    bands = bands_here * n_band
-    stacked = pieces.reshape(2 * bands, chunk)
-    prod = lax.dot_general(stacked, stacked, (((1,), (1,)), ((), ())), precision=HIGHEST)
-    gram_real = prod[:bands, :bands] + prod[bands:, bands:]
-    gram_imag = prod[:bands, bands:] - prod[bands:, :bands]
-    partial = jnp.stack([gram_real, gram_imag]).reshape(1, 2, n_band, bands_here, bands)
-    rows = lax.all_to_all(partial, "band", split_axis=2, concat_axis=0, tiled=True)
-    return jnp.sum(rows, axis=0).reshape(2, bands_here, bands)
+    me = lax.axis_index("band")
+    buffer = orbitals[None]
+    step = 1
+    while step < n_band:
+        pairs = [(i, i ^ step) for i in range(n_band)]
+        buffer = jnp.concatenate([buffer, lax.ppermute(buffer, "band", pairs)], axis=0)
+        step *= 2
+    prod = jnp.einsum("cbg,tefg->cbtfe", orbitals, buffer, precision=HIGHEST)
+    gram_real = prod[0, ..., 0] + prod[1, ..., 1]
+    gram_imag = prod[0, ..., 1] - prod[1, ..., 0]
+    slots = jnp.stack([gram_real, gram_imag])
+    held = lax.iota(jnp.int32, n_band) ^ me
+    rows = jnp.take(slots, held, axis=2)
+    return rows.reshape(2, bands_here, n_band * bands_here)
 
 
 def local(orbitals, pw_index, potential):

time: 95.9 us -> 107 us (1.12)
  starting transfers between devices: 33.9 us -> 42.4 us
  blocking collectives: 18 us -> 24.4 us
  waiting for transfers between devices: 26.9 us -> 20.8 us
  matrix products: 3.44 us -> 5.13 us
    ppermute x0 -> x5, starting transfers between devices: none -> 29.1 us  [gram_rows(): lax.ppermute(buffer, 'band', pairs)]
    all_to_all x2 -> x0, starting transfers between devices: 21.8 us -> none  [the longest x1 18 us: gram_rows(): lax.all_to_all(pieces, 'band', split_axis=2, concat_axis=1, tiled=True)]
    ppermute x0 -> x5, waiting for transfers between devices: none -> 20.8 us  [gram_rows(): lax.ppermute(buffer, 'band', pairs)]
    all_to_all x1, waiting for transfers between devices: 14.5 us -> 0.01 us  [local(): piece = lax.all_to_all(slab, 'pw', split_axis=3, concat_axis=1, tiled=True)]
    all_to_all x2 -> x0, waiting for transfers between devices: 12.4 us -> none  [the longest x1 7 us: gram_rows(): lax.all_to_all(partial, 'band', split_axis=2, concat_axis=0, tiled=True)]
    all_to_all x1, blocking collectives: 18 us -> 24.4 us  [local(): lax.all_to_all(payload, 'pw', split_axis=0, concat_axis=0, tiled=True)]
    dot_general x1, matrix products: 0.18 us -> 1.87 us  [gram_rows(): prod = jnp.einsum('cbg,tefg->cbtfe', orbitals, buffer, precision=HIGHEST)]
    reshape x3 -> x0, local copies, waits for them, and re-layouts: 1.37 us -> none  [the longest x2 0.74 us: gram_rows(): pieces = orbitals.reshape(2, bands_here, n_band, chunk)]
  transfers between devices with their start and end apart: 3 -> 6, of which waited for: 3 -> 3; matrix products, arithmetic and copies ran while one was open for 4% -> 6% of each run, Pallas kernels for 0% -> 0%
where the time goes in v3:
time: 107 us; the launch traced here: 106 us
  starting transfers between devices  42.4 us (40%)
  blocking collectives  24.4 us (23%)
  waiting for transfers between devices  20.8 us (19%)
  local copies, waits for them, and re-layouts  11.3 us (11%)
  matrix products  5.13 us (5%)
  other arithmetic  1.3 us (1%)
    ppermute x5, starting transfers between devices, gram_rows(): lax.ppermute(buffer, 'band', pairs)  29.1 us
    all_to_all x1, blocking collectives, local(): lax.all_to_all(payload, 'pw', split_axis=0, concat_axis=0, tiled=True)  24.4 us
    ppermute x5, waiting for transfers between devices, gram_rows(): lax.ppermute(buffer, 'band', pairs)  20.8 us
    all_to_all x1, starting transfers between devices, local(): piece = lax.all_to_all(slab, 'pw', split_axis=3, concat_axis=1, tiled=True)  13.2 us
    unnamed x17, local copies, waits for them, and re-layouts  4.72 us
    dot_general x6, matrix products, contract(): return jnp.einsum(form, values, table, precision=HIGHEST)  3.26 us
  transfers between devices with their start and end apart: 6, of which 3 were waited for; matrix products, arithmetic and copies ran while one was open for 6% of the time, Pallas kernels for 0%

profile of v3, /device:TPU:16, one launch (start us, length us, event | category | flops | bytes accessed | tf_op | source)
XLA Modules:
  0.0 106.4 jit_solution(15854611609130873951)
XLA Ops:
  0.6 1.9 %collective-permute-start = (f32[1,2,1,3456]{3,0,1,2:T(1,128)}, f32[1,2,1,3456]{3,0,1,2:T(1,128)S(1)}, u32[]{:S(2)}, u32[]{:S(2)}) collective-permute-start(f32[1,2,1,3456]{3,0,1,2:T(1,128)} %bitcast.79), channel_id=1, source_target_pairs={{0,32},{32,0},{64,96},{96,64},{128,160},{160,128},{192,224},{224,1... | collective-permute-start | bytes 82952 | tf_op jit(solution)/shard_map/ppermute | solution.py:39
  2.6 0.7 multiply_subtract_fusion
  3.6 0.7 copy-done
  4.4 0.3 reshape.187
  5.0 0.8 copy-done.6
  5.8 0.7 fusion.10
  6.8 5.2 %collective-permute-start.1 = (f32[2,2,1,3456]{3,0,1,2:T(2,128)S(1)}, f32[2,2,1,3456]{3,0,1,2:T(2,128)S(1)}, u32[]{:S(2)}, u32[]{:S(2)}) collective-permute-start(f32[2,2,1,3456]{3,0,1,2:T(2,128)S(1)} %pad_maximum_fusion.2), channel_id=1, source_target_pairs={{0,64},{32,96},{64,0},{96,32},{128,192},{160,224},{192,128},{224,1... | collective-permute-start | bytes 165896 | tf_op jit(solution)/shard_map/ppermute | solution.py:39
  12.0 0.5 fusion.11
  12.5 0.9 copy.31
  13.4 13.2 %all-to-all-start = ((f32[1,3,2,96,96]{4,2,1,0,3:T(2,128)}), f32[1,3,2,96,96]{4,2,1,0,3:T(2,128)S(1)}, u32[]{:S(2)}, u32[]{:S(2)}) async-start(f32[1,3,2,96,96]{4,2,1,0,3:T(2,128)} %copy.31), calls=%async_computation | async-start | bytes 589824 | tf_op jit(solution)/shard_map/all_to_all | solution.py:69
  26.7 7.7 %collective-permute-start.2 = (f32[4,2,1,3456]{3,0,1,2:T(4,128)S(1)}, f32[4,2,1,3456]{3,0,1,2:T(4,128)S(1)}, u32[]{:S(2)}, u32[]{:S(2)}) collective-permute-start(f32[4,2,1,3456]{3,0,1,2:T(4,128)S(1)} %pad_maximum_fusion.1), channel_id=1, source_target_pairs={{0,128},{32,160},{64,192},{96,224},{128,0},{160,32},{192,64},{224,... | collective-permute-start | bytes 331784 | tf_op jit(solution)/shard_map/ppermute | solution.py:39
  34.5 4.8 %collective-permute-done.2 = f32[4,2,1,3456]{3,0,1,2:T(4,128)S(1)} collective-permute-done((f32[4,2,1,3456]{3,0,1,2:T(4,128)S(1)}, f32[4,2,1,3456]{3,0,1,2:T(4,128)S(1)}, u32[]{:S(2)}, u32[]{:S(2)}) %collective-permute-start.2) | collective-permute-done | bytes 110624 | tf_op jit(solution)/shard_map/ppermute | solution.py:39
  39.5 11.9 %collective-permute-start.3 = (f32[8,2,1,3456]{3,0,1,2:T(8,128)S(1)}, f32[8,2,1,3456]{3,0,1,2:T(8,128)S(1)}, u32[]{:S(2)}, u32[]{:S(2)}) collective-permute-start(f32[8,2,1,3456]{3,0,1,2:T(8,128)S(1)} %pad_maximum_fusion), channel_id=1, source_target_pairs={{0,256},{32,288},{64,320},{96,352},{128,384},{160,416},{192,448},{... | collective-permute-start | bytes 663560 | tf_op jit(solution)/shard_map/ppermute | solution.py:39
  51.4 10.4 %collective-permute-done.3 = f32[8,2,1,3456]{3,0,1,2:T(8,128)S(1)} collective-permute-done((f32[8,2,1,3456]{3,0,1,2:T(8,128)S(1)}, f32[8,2,1,3456]{3,0,1,2:T(8,128)S(1)}, u32[]{:S(2)}, u32[]{:S(2)}) %collective-permute-start.3) | collective-permute-done | bytes 221216 | tf_op jit(solution)/shard_map/ppermute | solution.py:39
  61.9 2.5 %collective-permute-start.4 = (f32[16,2,1,3456]{3,0,1,2:T(8,128)S(1)}, f32[16,2,1,3456]{3,0,1,2:T(8,128)S(1)}, u32[]{:S(2)}, u32[]{:S(2)}) collective-permute-start(f32[16,2,1,3456]{3,0,1,2:T(8,128)S(1)} %concatenate.25), channel_id=1, source_target_pairs={{0,512},{32,544},{64,576},{96,608},{128,640},{160,672},{192,704},{... | collective-permute-start | bytes 1327112 | tf_op jit(solution)/shard_map/ppermute | solution.py:39
  64.6 0.8 copy-done.2
  65.5 0.5 convolution_multiply_fusion
  66.2 0.7 copy-done.4
  66.9 0.5 fusion.12
  67.8 5.6 %collective-permute-done.4 = f32[16,2,1,3456]{3,0,1,2:T(8,128)S(1)} collective-permute-done((f32[16,2,1,3456]{3,0,1,2:T(8,128)S(1)}, f32[16,2,1,3456]{3,0,1,2:T(8,128)S(1)}, u32[]{:S(2)}, u32[]{:S(2)}) %collective-permute-start.4) | collective-permute-done | bytes 442400 | tf_op jit(solution)/shard_map/ppermute | solution.py:39
  73.4 0.3 concatenate.26
  73.8 1.9 %convolution_bitcast_fusion.1 = f32[2,1,32,1,2]{2,0,1,3,4:T(2,128)S(1)} fusion(f32[32,2,1,3456]{3,0,1,2:T(8,128)S(1)} %concatenate.26, f32[2,1,3456]{2,1,0:T(1,128)S(1)} %copy-done), kind=kOutput, calls=%fused_computation.5 | convolution fusion | flops 5308416 | bytes 912896 | tf_op jit(solution)/shard_map/cbg,tefg->cbtfe/dot_general | solution.py:41
  75.8 0.6 gather_fusion
  76.6 0.2 copy.38
  76.9 24.4 %all_to_all.27 = f32[32,1,1792]{2,1,0:T(1,128)S(1)} all-to-all(f32[32,1,1792]{2,1,0:T(1,128)S(1)} %copy.38), channel_id=1, replica_groups=mesh['band'=32,'pw'=32] {'pw'}, dimensions={0} | all-to-all | bytes 458752 | tf_op jit(solution)/shard_map/all_to_all | solution.py:81
  101.4 0.3 reshape.194
  102.0 0.8 copy-done.3
  102.7 0.5 convolution_bitcast_fusion
  103.3 0.8 copy-done.1
  104.2 0.6 fusion
  104.9 0.9 reshape.228
  105.8 0.6 div.10
  (50 shorter events, 3.1 us)
Async XLA Ops:
  0.6 6.1 %collective-permute-start = (f32[1,2,1,3456]{3,0,1,2:T(1,128)}, f32[1,2,1,3456]{3,0,1,2:T(1,128)S(1)}, u32[]{:S(2)}, u32[]{:S(2)}) collective-permute-start(f32[1,2,1,3456]{3,0,1,2:T(1,128)} %bitcast.79), channel_id=1, source_target_pairs={{0,32},{32,0},{64,96},{96,64},{128,160},{160,128},{192,224},{224,1... | collective-permute-start | bytes 82952 | tf_op jit(solution)/shard_map/ppermute | solution.py:39
  3.5 0.8 copy-start
  4.9 0.9 copy-start.6
  6.6 5.4 %copy-start.5 = (f32[192,192,1]{0,1,2:T(8,128)S(1)}, f32[192,192,1]{0,1,2:T(8,128)}, u32[]{:S(2)}) copy-start(f32[192,192,1]{0,1,2:T(8,128)} %constant.58) | copy-start | bytes 442372
  6.8 19.9 %collective-permute-start.1 = (f32[2,2,1,3456]{3,0,1,2:T(2,128)S(1)}, f32[2,2,1,3456]{3,0,1,2:T(2,128)S(1)}, u32[]{:S(2)}, u32[]{:S(2)}) collective-permute-start(f32[2,2,1,3456]{3,0,1,2:T(2,128)S(1)} %pad_maximum_fusion.2), channel_id=1, source_target_pairs={{0,64},{32,96},{64,0},{96,32},{128,192},{160,224},{192,128},{224,1... | collective-permute-start | bytes 165896 | tf_op jit(solution)/shard_map/ppermute | solution.py:39
  13.4 51.0 %all-to-all-start = ((f32[1,3,2,96,96]{4,2,1,0,3:T(2,128)}), f32[1,3,2,96,96]{4,2,1,0,3:T(2,128)S(1)}, u32[]{:S(2)}, u32[]{:S(2)}) async-start(f32[1,3,2,96,96]{4,2,1,0,3:T(2,128)} %copy.31), calls=%async_computation | async-start | bytes 589824 | tf_op jit(solution)/shard_map/all_to_all | solution.py:69
  26.7 12.6 %collective-permute-start.2 = (f32[4,2,1,3456]{3,0,1,2:T(4,128)S(1)}, f32[4,2,1,3456]{3,0,1,2:T(4,128)S(1)}, u32[]{:S(2)}, u32[]{:S(2)}) collective-permute-start(f32[4,2,1,3456]{3,0,1,2:T(4,128)S(1)} %pad_maximum_fusion.1), channel_id=1, source_target_pairs={{0,128},{32,160},{64,192},{96,224},{128,0},{160,32},{192,64},{224,... | collective-permute-start | bytes 331784 | tf_op jit(solution)/shard_map/ppermute | solution.py:39
  39.5 22.2 %collective-permute-start.3 = (f32[8,2,1,3456]{3,0,1,2:T(8,128)S(1)}, f32[8,2,1,3456]{3,0,1,2:T(8,128)S(1)}, u32[]{:S(2)}, u32[]{:S(2)}) collective-permute-start(f32[8,2,1,3456]{3,0,1,2:T(8,128)S(1)} %pad_maximum_fusion), channel_id=1, source_target_pairs={{0,256},{32,288},{64,320},{96,352},{128,384},{160,416},{192,448},{... | collective-permute-start | bytes 663560 | tf_op jit(solution)/shard_map/ppermute | solution.py:39
  61.9 11.5 %collective-permute-start.4 = (f32[16,2,1,3456]{3,0,1,2:T(8,128)S(1)}, f32[16,2,1,3456]{3,0,1,2:T(8,128)S(1)}, u32[]{:S(2)}, u32[]{:S(2)}) collective-permute-start(f32[16,2,1,3456]{3,0,1,2:T(8,128)S(1)} %concatenate.25), channel_id=1, source_target_pairs={{0,512},{32,544},{64,576},{96,608},{128,640},{160,672},{192,704},{... | collective-permute-start | bytes 1327112 | tf_op jit(solution)/shard_map/ppermute | solution.py:39
  64.5 0.9 copy-start.2
  64.5 1.0 copy-start.7
  66.0 0.9 copy-start.4
  101.8 0.9 copy-start.3
  103.2 1.0 copy-start.1

commit v4 on v2

--- a/solution.py
+++ b/solution.py
@@ -39,9 +39,26 @@
     prod = lax.dot_general(stacked, stacked, (((1,), (1,)), ((), ())), precision=HIGHEST)
     gram_real = prod[:bands, :bands] + prod[bands:, bands:]
     gram_imag = prod[:bands, bands:] - prod[bands:, :bands]
-    partial = jnp.stack([gram_real, gram_imag]).reshape(1, 2, n_band, bands_here, bands)
-    rows = lax.all_to_all(partial, "band", split_axis=2, concat_axis=0, tiled=True)
-    return jnp.sum(rows, axis=0).reshape(2, bands_here, bands)
+    partial = jnp.stack([gram_real, gram_imag]).reshape(2, n_band, bands_here, bands)
+    return scatter_rows(jnp.transpose(partial, (1, 0, 2, 3)))
+
+
+def scatter_rows(blocks):
+    n_band = blocks.shape[0]
+    me = lax.axis_index("band")
+    bits = n_band.bit_length() - 1
+    assert 1 << bits == n_band
+    buffer = blocks.reshape((2,) * bits + blocks.shape[1:])
+    for bit in range(bits):
+        axis = bits - 1 - bit
+        mine = (me >> bit) & 1
+        low = lax.index_in_dim(buffer, 0, axis, keepdims=False)
+        high = lax.index_in_dim(buffer, 1, axis, keepdims=False)
+        keep = jnp.where(mine == 1, high, low)
+        send = jnp.where(mine == 1, low, high)
+        pairs = [(i, i ^ (1 << bit)) for i in range(n_band)]
+        buffer = keep + lax.ppermute(send, "band", pairs)
+    return buffer
 
 
 def local(orbitals, pw_index, potential):

time: 95.9 us -> 99.8 us (1.041)
  starting transfers between devices: 33.9 us -> 42.1 us
  waiting for transfers between devices: 26.9 us -> 24.9 us
  local copies, waits for them, and re-layouts: 11 us -> 9.26 us
    ppermute x0 -> x5, starting transfers between devices: none -> 12 us  [scatter_rows(): buffer = keep + lax.ppermute(send, 'band', pairs)]
    ppermute x0 -> x5, waiting for transfers between devices: none -> 9.5 us  [scatter_rows(): buffer = keep + lax.ppermute(send, 'band', pairs)]
    all_to_all x1, waiting for transfers between devices: 14.5 us -> 7.25 us  [local(): piece = lax.all_to_all(slab, 'pw', split_axis=3, concat_axis=1, tiled=True)]
    all_to_all x1 -> x0, waiting for transfers between devices: 7 us -> none  [gram_rows(): lax.all_to_all(partial, 'band', split_axis=2, concat_axis=0, tiled=True)]
    all_to_all x1 -> x0, starting transfers between devices: 3.8 us -> none  [gram_rows(): lax.all_to_all(partial, 'band', split_axis=2, concat_axis=0, tiled=True)]
    all_to_all x1, waiting for transfers between devices: 5.43 us -> 8.16 us  [gram_rows(): lax.all_to_all(pieces, 'band', split_axis=2, concat_axis=1, tiled=True)]
    unnamed x17, local copies, waits for them, and re-layouts: 4.39 us -> 3.2 us
  transfers between devices with their start and end apart: 3 -> 7, of which waited for: 3 -> 6; matrix products, arithmetic and copies ran while one was open for 4% -> 3% of each run, Pallas kernels for 0% -> 0%
where the time goes in v4:
time: 99.8 us; the launch traced here: 99.1 us
  starting transfers between devices  42.1 us (42%)
  waiting for transfers between devices  24.9 us (25%)
  blocking collectives  17.1 us (17%)
  local copies, waits for them, and re-layouts  9.26 us (9%)
  matrix products  3.45 us (3%)
  other arithmetic  1.18 us (1%)
  between operations  1.07 us (1%)
    all_to_all x1, starting transfers between devices, gram_rows(): lax.all_to_all(pieces, 'band', split_axis=2, concat_axis=1, tiled=True)  18.1 us
    all_to_all x1, blocking collectives, local(): lax.all_to_all(payload, 'pw', split_axis=0, concat_axis=0, tiled=True)  17.1 us
    all_to_all x1, starting transfers between devices, local(): piece = lax.all_to_all(slab, 'pw', split_axis=3, concat_axis=1, tiled=True)  12.1 us
    ppermute x5, starting transfers between devices, scatter_rows(): buffer = keep + lax.ppermute(send, 'band', pairs)  12 us
    ppermute x5, waiting for transfers between devices, scatter_rows(): buffer = keep + lax.ppermute(send, 'band', pairs)  9.5 us
    all_to_all x1, waiting for transfers between devices, gram_rows(): lax.all_to_all(pieces, 'band', split_axis=2, concat_axis=1, tiled=True)  8.16 us
    all_to_all x1, waiting for transfers between devices, local(): piece = lax.all_to_all(slab, 'pw', split_axis=3, concat_axis=1, tiled=True)  7.25 us
    dot_general x6, matrix products, contract(): return jnp.einsum(form, values, table, precision=HIGHEST)  3.27 us
  transfers between devices with their start and end apart: 7, of which 6 were waited for; matrix products, arithmetic and copies ran while one was open for 3% of the time, Pallas kernels for 0%

profile of v4, /device:TPU:16, one launch (start us, length us, event | category | flops | bytes accessed | tf_op | source)
XLA Modules:
  0.0 99.1 jit_solution(17342079081513647008)
XLA Ops:
  0.6 0.8 reduce.2
  1.6 0.6 copy.61
  2.2 18.1 %all-to-all-start.1 = ((f32[2,1,32,108]{3,0,1,2:T(2,128)}), f32[2,1,32,108]{3,0,1,2:T(2,128)S(1)}, u32[]{:S(2)}, u32[]{:S(2)}) async-start(f32[2,1,32,108]{3,0,1,2:T(2,128)} %copy.61), calls=%async_computation.1 | async-start | bytes 65536 | tf_op jit(solution)/shard_map/all_to_all | solution.py:36
  20.6 8.2 %all-to-all-done.1 = f32[2,1,32,108]{3,0,1,2:T(2,128)S(1)} async-done(((f32[2,1,32,108]{3,0,1,2:T(2,128)}), f32[2,1,32,108]{3,0,1,2:T(2,128)S(1)}, u32[]{:S(2)}, u32[]{:S(2)}) %all-to-all-start.1) | async-done | bytes 27680 | tf_op jit(solution)/shard_map/all_to_all | solution.py:36
  29.1 1.9 %collective-permute-start = (f32[2,2,2,2,2,1,32]{6,4,0,1,2,5,3:T(2,128)S(1)}, f32[2,2,2,2,2,1,32]{6,4,0,1,2,5,3:T(2,128)S(1)}, u32[]{:S(2)}, u32[]{:S(2)}) collective-permute-start(f32[2,2,2,2,2,1,32]{6,4,0,1,2,5,3:T(2,128)S(1)} %select_bitcast_fusion), channel_id=1, source_target_pairs={{0,32},{32,0},{64,96},{96,64},{128,160},{160,128},{192,224},{224,1... | collective-permute-start | bytes 12296 | tf_op jit(solution)/shard_map/ppermute | solution.py:60
  31.1 0.3 reshape.337
  31.6 0.7 collective-permute-done
  32.3 2.5 %collective-permute-start.1 = (f32[2,2,2,2,1,32]{5,3,0,1,4,2:T(2,128)S(1)}, f32[2,2,2,2,1,32]{5,3,0,1,4,2:T(2,128)S(1)}, u32[]{:S(2)}, u32[]{:S(2)}) collective-permute-start(f32[2,2,2,2,1,32]{5,3,0,1,4,2:T(2,128)S(1)} %select_bitcast_fusion.1), channel_id=1, source_target_pairs={{0,64},{32,96},{64,0},{96,32},{128,192},{160,224},{192,128},{224,1... | collective-permute-start | bytes 6152 | tf_op jit(solution)/shard_map/ppermute | solution.py:60
  34.9 2.9 %collective-permute-done.1 = f32[2,2,2,2,1,32]{5,3,0,1,4,2:T(2,128)S(1)} collective-permute-done((f32[2,2,2,2,1,32]{5,3,0,1,4,2:T(2,128)S(1)}, f32[2,2,2,2,1,32]{5,3,0,1,4,2:T(2,128)S(1)}, u32[]{:S(2)}, u32[]{:S(2)}) %collective-permute-start.1) | collective-permute-done | bytes 2080 | tf_op jit(solution)/shard_map/ppermute | solution.py:60
  37.8 2.5 %collective-permute-start.2 = (f32[2,2,2,1,32]{4,2,0,3,1:T(2,128)S(1)}, f32[2,2,2,1,32]{4,2,0,3,1:T(2,128)S(1)}, u32[]{:S(2)}, u32[]{:S(2)}) collective-permute-start(f32[2,2,2,1,32]{4,2,0,3,1:T(2,128)S(1)} %select_bitcast_fusion.2), channel_id=1, source_target_pairs={{0,128},{32,160},{64,192},{96,224},{128,0},{160,32},{192,64},{224,... | collective-permute-start | bytes 3080 | tf_op jit(solution)/shard_map/ppermute | solution.py:60
  40.3 0.7 fusion.7
  41.2 3.0 %collective-permute-done.2 = f32[2,2,2,1,32]{4,2,0,3,1:T(2,128)S(1)} collective-permute-done((f32[2,2,2,1,32]{4,2,0,3,1:T(2,128)S(1)}, f32[2,2,2,1,32]{4,2,0,3,1:T(2,128)S(1)}, u32[]{:S(2)}, u32[]{:S(2)}) %collective-permute-start.2) | collective-permute-done | bytes 1056 | tf_op jit(solution)/shard_map/ppermute | solution.py:60
  44.3 2.5 %collective-permute-start.3 = (f32[2,2,1,32]{3,1,0,2:T(2,128)S(1)}, f32[2,2,1,32]{3,1,0,2:T(2,128)S(1)}, u32[]{:S(2)}, u32[]{:S(2)}) collective-permute-start(f32[2,2,1,32]{3,1,0,2:T(2,128)S(1)} %select_bitcast_fusion.3), channel_id=1, source_target_pairs={{0,256},{32,288},{64,320},{96,352},{128,384},{160,416},{192,448},{... | collective-permute-start | bytes 1544 | tf_op jit(solution)/shard_map/ppermute | solution.py:60
  46.8 0.5 fusion.8
  47.2 0.9 copy.56
  48.2 12.1 %all-to-all-start = ((f32[1,3,2,96,96]{4,2,1,0,3:T(2,128)}), f32[1,3,2,96,96]{4,2,1,0,3:T(2,128)S(1)}, u32[]{:S(2)}, u32[]{:S(2)}) async-start(f32[1,3,2,96,96]{4,2,1,0,3:T(2,128)} %copy.56), calls=%async_computation | async-start | bytes 589824 | tf_op jit(solution)/shard_map/all_to_all | solution.py:83
  60.3 2.6 %collective-permute-start.4 = (f32[2,1,32]{2,0,1:T(2,128)S(1)}, f32[2,1,32]{2,0,1:T(2,128)S(1)}, u32[]{:S(2)}, u32[]{:S(2)}) collective-permute-start(f32[2,1,32]{2,0,1:T(2,128)S(1)} %select_bitcast_fusion.4), channel_id=1, source_target_pairs={{0,512},{32,544},{64,576},{96,608},{128,640},{160,672},{192,704},{... | collective-permute-start | bytes 776 | tf_op jit(solution)/shard_map/ppermute | solution.py:60
  62.9 2.9 %collective-permute-done.4 = f32[2,1,32]{2,0,1:T(2,128)S(1)} collective-permute-done((f32[2,1,32]{2,0,1:T(2,128)S(1)}, f32[2,1,32]{2,0,1:T(2,128)S(1)}, u32[]{:S(2)}, u32[]{:S(2)}) %collective-permute-start.4) | collective-permute-done | bytes 288 | tf_op jit(solution)/shard_map/ppermute | solution.py:60
  66.0 7.2 %all-to-all-done = f32[1,3,2,96,96]{4,2,1,0,3:T(2,128)S(1)} async-done(((f32[1,3,2,96,96]{4,2,1,0,3:T(2,128)}), f32[1,3,2,96,96]{4,2,1,0,3:T(2,128)S(1)}, u32[]{:S(2)}, u32[]{:S(2)}) %all-to-all-start) | async-done | bytes 221216 | tf_op jit(solution)/shard_map/all_to_all | solution.py:83
  73.4 0.8 copy-done.1
  74.3 0.5 convolution_multiply_fusion
  75.0 0.7 copy-done.3
  75.7 0.5 fusion.9
  76.6 0.2 copy.68
  76.9 17.1 %all_to_all.36 = f32[32,1,1792]{2,1,0:T(1,128)S(1)} all-to-all(f32[32,1,1792]{2,1,0:T(1,128)S(1)} %copy.68), channel_id=1, replica_groups=mesh['band'=32,'pw'=32] {'pw'}, dimensions={0} | all-to-all | bytes 458752 | tf_op jit(solution)/shard_map/all_to_all | solution.py:95
  94.1 0.6 div.10
  94.8 0.3 reshape.346
  95.3 0.8 copy-done.2
  96.1 0.5 convolution_bitcast_fusion
  96.7 0.8 copy-done
  97.5 0.6 fusion
  98.3 0.9 reshape.363
  (52 shorter events, 2.8 us)
Async XLA Ops:
  2.2 18.1 %copy-start.7 = (s32[3456]{0:T(1024)S(1)}, s32[3456]{0:T(1024)}, u32[]{:S(2)}) copy-start(s32[3456]{0:T(1024)} %param.10) | copy-start | bytes 41476
  2.2 26.6 %all-to-all-start.1 = ((f32[2,1,32,108]{3,0,1,2:T(2,128)}), f32[2,1,32,108]{3,0,1,2:T(2,128)S(1)}, u32[]{:S(2)}, u32[]{:S(2)}) async-start(f32[2,1,32,108]{3,0,1,2:T(2,128)} %copy.61), calls=%async_computation.1 | async-start | bytes 65536 | tf_op jit(solution)/shard_map/all_to_all | solution.py:36
  29.1 3.1 %collective-permute-start = (f32[2,2,2,2,2,1,32]{6,4,0,1,2,5,3:T(2,128)S(1)}, f32[2,2,2,2,2,1,32]{6,4,0,1,2,5,3:T(2,128)S(1)}, u32[]{:S(2)}, u32[]{:S(2)}) collective-permute-start(f32[2,2,2,2,2,1,32]{6,4,0,1,2,5,3:T(2,128)S(1)} %select_bitcast_fusion), channel_id=1, source_target_pairs={{0,32},{32,0},{64,96},{96,64},{128,160},{160,128},{192,224},{224,1... | collective-permute-start | bytes 12296 | tf_op jit(solution)/shard_map/ppermute | solution.py:60
  32.3 5.5 %collective-permute-start.1 = (f32[2,2,2,2,1,32]{5,3,0,1,4,2:T(2,128)S(1)}, f32[2,2,2,2,1,32]{5,3,0,1,4,2:T(2,128)S(1)}, u32[]{:S(2)}, u32[]{:S(2)}) collective-permute-start(f32[2,2,2,2,1,32]{5,3,0,1,4,2:T(2,128)S(1)} %select_bitcast_fusion.1), channel_id=1, source_target_pairs={{0,64},{32,96},{64,0},{96,32},{128,192},{160,224},{192,128},{224,1... | collective-permute-start | bytes 6152 | tf_op jit(solution)/shard_map/ppermute | solution.py:60
  34.8 5.5 %copy-start.5 = (f32[192,192,1]{1,0,2:T(8,128)S(1)}, f32[192,192,1]{1,0,2:T(8,128)}, u32[]{:S(2)}) copy-start(f32[192,192,1]{1,0,2:T(8,128)} %constant.53) | copy-start | bytes 442372
  37.8 6.4 %collective-permute-start.2 = (f32[2,2,2,1,32]{4,2,0,3,1:T(2,128)S(1)}, f32[2,2,2,1,32]{4,2,0,3,1:T(2,128)S(1)}, u32[]{:S(2)}, u32[]{:S(2)}) collective-permute-start(f32[2,2,2,1,32]{4,2,0,3,1:T(2,128)S(1)} %select_bitcast_fusion.2), channel_id=1, source_target_pairs={{0,128},{32,160},{64,192},{96,224},{128,0},{160,32},{192,64},{224,... | collective-permute-start | bytes 3080 | tf_op jit(solution)/shard_map/ppermute | solution.py:60
  41.1 5.7 %copy-start.4 = (f32[192,192,1]{0,1,2:T(8,128)S(1)}, f32[192,192,1]{0,1,2:T(8,128)}, u32[]{:S(2)}) copy-start(f32[192,192,1]{0,1,2:T(8,128)} %constant.52) | copy-start | bytes 442372
  44.3 16.0 %collective-permute-start.3 = (f32[2,2,1,32]{3,1,0,2:T(2,128)S(1)}, f32[2,2,1,32]{3,1,0,2:T(2,128)S(1)}, u32[]{:S(2)}, u32[]{:S(2)}) collective-permute-start(f32[2,2,1,32]{3,1,0,2:T(2,128)S(1)} %select_bitcast_fusion.3), channel_id=1, source_target_pairs={{0,256},{32,288},{64,320},{96,352},{128,384},{160,416},{192,448},{... | collective-permute-start | bytes 1544 | tf_op jit(solution)/shard_map/ppermute | solution.py:60
  48.2 25.0 %all-to-all-start = ((f32[1,3,2,96,96]{4,2,1,0,3:T(2,128)}), f32[1,3,2,96,96]{4,2,1,0,3:T(2,128)S(1)}, u32[]{:S(2)}, u32[]{:S(2)}) async-start(f32[1,3,2,96,96]{4,2,1,0,3:T(2,128)} %copy.56), calls=%async_computation | async-start | bytes 589824 | tf_op jit(solution)/shard_map/all_to_all | solution.py:83
  60.3 5.5 %collective-permute-start.4 = (f32[2,1,32]{2,0,1:T(2,128)S(1)}, f32[2,1,32]{2,0,1:T(2,128)S(1)}, u32[]{:S(2)}, u32[]{:S(2)}) collective-permute-start(f32[2,1,32]{2,0,1:T(2,128)S(1)} %select_bitcast_fusion.4), channel_id=1, source_target_pairs={{0,512},{32,544},{64,576},{96,608},{128,640},{160,672},{192,704},{... | collective-permute-start | bytes 776 | tf_op jit(solution)/shard_map/ppermute | solution.py:60
  73.2 0.9 copy-start.1
  73.3 1.0 %copy-start.6 = (f32[96,3,96]{2,0,1:T(8,128)S(1)}, f32[96,3,96]{2,0,1:T(8,128)}, u32[]{:S(2)}) copy-start(f32[96,3,96]{2,0,1:T(8,128)} %param.11) | copy-start | bytes 331780
  74.7 0.9 copy-start.3
  95.2 0.9 copy-start.2
  96.6 1.0 copy-start

commit v5 on v2

--- a/solution.py
+++ b/solution.py
@@ -28,20 +28,26 @@
     return jnp.einsum(form, values, table, precision=HIGHEST)
 
 
+def exchange(blocks, axis):
+    n = blocks.shape[0]
+    flat = lax.all_to_all(blocks.reshape(n, -1), axis, split_axis=0, concat_axis=0, tiled=True)
+    return flat.reshape(blocks.shape)
+
+
 def gram_rows(orbitals):
     _, bands_here, columns = orbitals.shape
     n_band = lax.axis_size("band")
     chunk = columns // n_band
-    pieces = orbitals.reshape(2, bands_here, n_band, chunk)
-    pieces = lax.all_to_all(pieces, "band", split_axis=2, concat_axis=1, tiled=True)
+    pieces = jnp.transpose(orbitals.reshape(2, bands_here, n_band, chunk), (2, 0, 1, 3))
+    pieces = exchange(pieces, "band")
     bands = bands_here * n_band
-    stacked = pieces.reshape(2 * bands, chunk)
+    stacked = jnp.transpose(pieces, (1, 0, 2, 3)).reshape(2 * bands, chunk)
     prod = lax.dot_general(stacked, stacked, (((1,), (1,)), ((), ())), precision=HIGHEST)
     gram_real = prod[:bands, :bands] + prod[bands:, bands:]
     gram_imag = prod[:bands, bands:] - prod[bands:, :bands]
-    partial = jnp.stack([gram_real, gram_imag]).reshape(1, 2, n_band, bands_here, bands)
-    rows = lax.all_to_all(partial, "band", split_axis=2, concat_axis=0, tiled=True)
-    return jnp.sum(rows, axis=0).reshape(2, bands_here, bands)
+    partial = jnp.stack([gram_real, gram_imag]).reshape(2, n_band, bands_here, bands)
+    rows = exchange(jnp.transpose(partial, (1, 0, 2, 3)), "band")
+    return jnp.sum(rows, axis=0)
 
 
 def local(orbitals, pw_index, potential):
@@ -52,7 +58,6 @@
     offsets = (pw_index - 8 * lax.iota(jnp.int32, columns)).reshape(planes, grid, blocks)
     lanes = lax.iota(jnp.int32, 8)
     hit = offsets[..., None] == lanes
-    rows = gram_rows(orbitals)
 
     coeffs = orbitals.reshape(2, bands_here, planes, grid, blocks)
     coeffs = jnp.transpose(coeffs, (1, 2, 3, 0, 4))
@@ -62,14 +67,19 @@
     slab = contract(spread, dft_table(grid, True, "ck", "dn"), "bxyw,wv->bxyv")
     slab = slab.reshape(bands_here, planes, 2 * grid, grid)
     slab = contract(slab, dft_table(grid, True, "kc", "dn"), "bxwz,wv->bxvz")
-    slab = slab.reshape(bands_here, planes, 2, grid, grid)
-    piece = lax.all_to_all(slab, "pw", split_axis=3, concat_axis=1, tiled=True)
+    slab, orbitals = lax.optimization_barrier((slab, orbitals))
+    rows = gram_rows(orbitals)
+    slab, rows = lax.optimization_barrier((slab, rows))
+    n_pw = lax.axis_size("pw")
+    slab = slab.reshape(bands_here, planes, 2, n_pw, planes, grid)
+    piece = exchange(jnp.transpose(slab, (3, 0, 1, 2, 4, 5)), "pw")
+    piece, rows = lax.optimization_barrier((piece, rows))
+    piece = jnp.transpose(piece, (1, 0, 2, 3, 4, 5))
     piece = piece.reshape(bands_here, 2 * grid, planes, grid)
     piece = contract(piece, dft_table(grid, True, "kc", "nd"), "bwyz,wv->bvyz")
     piece = piece.reshape(bands_here, grid, 2, planes, grid) * potential[None, :, None]
     piece = piece.reshape(bands_here, 2 * grid, planes, grid)
     piece = contract(piece, dft_table(grid, False, "kc", "nd"), "bwyz,wv->bvyz")
-    n_pw = lax.axis_size("pw")
     width = planes * 2 * planes * grid
     payload = piece.reshape(bands_here, n_pw, width).transpose(1, 0, 2)
     payload = payload.reshape(n_pw, bands_here * width)

time: 95.9 us -> 98.2 us (1.024)
  blocking collectives: 18 us -> 80.7 us
  starting transfers between devices: 33.9 us -> 0 us
  waiting for transfers between devices: 26.9 us -> 0 us
    all_to_all x0 -> x3, blocking collectives: none -> 62.8 us  [exchange(): lax.all_to_all(blocks.reshape(n, -1), axis, split_axis=0, concat_axis=0,...]
    all_to_all x3 -> x0, starting transfers between devices: 33.9 us -> none  [the longest x1 18 us: gram_rows(): lax.all_to_all(pieces, 'band', split_axis=2, concat_axis=1, tiled=True)]
    all_to_all x3 -> x0, waiting for transfers between devices: 26.9 us -> none  [the longest x1 14.5 us: local(): piece = lax.all_to_all(slab, 'pw', split_axis=3, concat_axis=1, tiled=True)]
    reshape x4, local copies, waits for them, and re-layouts: 2.31 us -> 0.54 us  [the longest x2 0.4 us: exchange(): return flat.reshape(blocks.shape)]
  transfers between devices with their start and end apart: 3 -> 0, of which waited for: 3 -> 0; matrix products, arithmetic and copies ran while one was open for 4% -> 0% of each run, Pallas kernels for 0% -> 0%
where the time goes in v5:
time: 98.2 us; the launch traced here: 97.7 us
  blocking collectives  80.7 us (82%)
  local copies, waits for them, and re-layouts  10.8 us (11%)
  matrix products  3.44 us (4%)
  other arithmetic  1.83 us (2%)
    all_to_all x3, blocking collectives, exchange(): lax.all_to_all(blocks.reshape(n, -1), axis, split_axis=0, concat_axis=0,...  62.8 us
    all_to_all x1, blocking collectives, local(): lax.all_to_all(payload, 'pw', split_axis=0, concat_axis=0, tiled=True)  17.8 us
    unnamed x17, local copies, waits for them, and re-layouts  5.26 us
    dot_general x6, matrix products, contract(): return jnp.einsum(form, values, table, precision=HIGHEST)  3.26 us

profile of v5, /device:TPU:16, one launch (start us, length us, event | category | flops | bytes accessed | tf_op | source)
XLA Modules:
  0.0 97.7 jit_solution(7186723477416195665)
XLA Ops:
  0.6 0.7 multiply_subtract_fusion
  1.4 0.2 eq.19
  1.7 0.7 copy-done.7
  2.5 0.3 reshape.132
  3.1 0.8 copy-done.5
  3.9 0.7 fusion.6
  4.8 0.8 copy-done.4
  5.6 0.5 convolution_bitcast_fusion.1
  6.4 26.2 %all_to_all.41 = f32[32,1,216]{2,1,0:T(1,128)S(1)} all-to-all(f32[32,1,216]{2,1,0:T(1,128)S(1)} %all_to_all.35), channel_id=1, replica_groups=mesh['band'=32,'pw'=32] {'band'}, dimensions={0} | all-to-all | bytes 55296 | tf_op jit(solution)/shard_map/all_to_all | solution.py:33
  32.8 0.2 fusion.7
  33.2 11.3 %all_to_all.42 = f32[32,1,64]{2,1,0:T(1,128)S(1)} all-to-all(f32[32,1,64]{2,1,0:T(1,128)S(1)} %bitcast.94), channel_id=1, replica_groups=mesh['band'=32,'pw'=32] {'band'}, dimensions={0} | all-to-all | bytes 16384 | tf_op jit(solution)/shard_map/all_to_all | solution.py:33
  44.8 0.5 all_to_all.36
  45.2 25.3 %all_to_all.43 = f32[32,1,1728]{2,1,0:T(1,128)S(1)} all-to-all(f32[32,1,1728]{2,1,0:T(1,128)S(1)} %all_to_all.36), channel_id=1, replica_groups=mesh['band'=32,'pw'=32] {'pw'}, dimensions={0} | all-to-all | bytes 442368 | tf_op jit(solution)/shard_map/all_to_all | solution.py:33
  70.5 0.5 reduce.8
  71.1 0.3 reshape.139
  71.4 0.6 copy-done.1
  72.0 0.5 convolution_multiply_fusion
  72.5 0.2 copy.57
  72.9 0.6 copy-done.3
  73.5 0.5 fusion.8
  73.9 0.2 copy.58
  74.2 0.2 transpose.49
  74.5 0.2 copy.59
  74.7 17.8 %all_to_all.44 = f32[32,1,1792]{2,1,0:T(1,128)S(1)} all-to-all(f32[32,1,1792]{2,1,0:T(1,128)S(1)} %copy.59), channel_id=1, replica_groups=mesh['band'=32,'pw'=32] {'pw'}, dimensions={0} | all-to-all | bytes 458752 | tf_op jit(solution)/shard_map/all_to_all | solution.py:88
  92.7 0.6 div.10
  93.3 0.3 reshape.142
  93.9 0.8 copy-done.2
  94.6 0.5 convolution_bitcast_fusion
  95.3 0.8 copy-done
  96.1 0.6 fusion
  96.7 0.1 copy.61
  96.9 0.9 reshape.155
  (39 shorter events, 2.2 us)
Async XLA Ops:
  1.6 0.8 copy-start.7
  3.0 0.9 copy-start.5
  4.6 0.9 copy-start.4
  71.0 0.9 copy-start.1
  71.0 1.0 %copy-start.6 = (f32[96,3,96]{2,0,1:T(8,128)S(1)}, f32[96,3,96]{2,0,1:T(8,128)}, u32[]{:S(2)}) copy-start(f32[96,3,96]{2,0,1:T(8,128)} %param.11) | copy-start | bytes 331780
  72.5 0.9 copy-start.3
  93.7 0.9 copy-start.2
  95.1 1.0 copy-start

commit v6 on v2

--- a/solution.py
+++ b/solution.py
@@ -4,7 +4,7 @@
 import numpy as np
 import jax.numpy as jnp
 from jax import lax
-from jax.sharding import PartitionSpec as P
+from jax.sharding import Mesh, PartitionSpec as P
 
 HIGHEST = lax.Precision.HIGHEST
 
@@ -26,6 +26,23 @@
 
 def contract(values, table, form):
     return jnp.einsum(form, values, table, precision=HIGHEST)
+
+
+def exchange(blocks, axis):
+    n = blocks.shape[0]
+    flat = lax.all_to_all(blocks.reshape(n, -1), axis, split_axis=0, concat_axis=0, tiled=True)
+    return flat.reshape(blocks.shape)
+
+
+def exchange_with_rows(blocks, rows, axis):
+    n = blocks.shape[0]
+    flat = blocks.reshape(n, -1)
+    width = flat.shape[1]
+    extra = jnp.broadcast_to(rows.reshape(1, -1), (n, rows.size))
+    flat = jnp.concatenate([flat, extra], axis=1)
+    flat = lax.all_to_all(flat, axis, split_axis=0, concat_axis=0, tiled=True)
+    total = jnp.sum(flat[:, width:], axis=0).reshape(rows.shape)
+    return flat[:, :width].reshape(blocks.shape), total
 
 
 def gram_rows(orbitals):
@@ -62,24 +79,21 @@
     slab = contract(spread, dft_table(grid, True, "ck", "dn"), "bxyw,wv->bxyv")
     slab = slab.reshape(bands_here, planes, 2 * grid, grid)
     slab = contract(slab, dft_table(grid, True, "kc", "dn"), "bxwz,wv->bxvz")
-    slab = slab.reshape(bands_here, planes, 2, grid, grid)
-    piece = lax.all_to_all(slab, "pw", split_axis=3, concat_axis=1, tiled=True)
+    n_hi, n_lo = lax.axis_size("pw_hi"), lax.axis_size("pw_lo")
+    slab = slab.reshape(bands_here, planes, 2, n_hi, n_lo, planes, grid)
+    slab = exchange(jnp.transpose(slab, (4, 0, 1, 2, 3, 5, 6)), "pw_lo")
+    slab = exchange(jnp.transpose(slab, (4, 0, 1, 2, 3, 5, 6)), "pw_hi")
+    piece = jnp.transpose(slab, (2, 0, 1, 3, 4, 5, 6))
     piece = piece.reshape(bands_here, 2 * grid, planes, grid)
     piece = contract(piece, dft_table(grid, True, "kc", "nd"), "bwyz,wv->bvyz")
     piece = piece.reshape(bands_here, grid, 2, planes, grid) * potential[None, :, None]
     piece = piece.reshape(bands_here, 2 * grid, planes, grid)
     piece = contract(piece, dft_table(grid, False, "kc", "nd"), "bwyz,wv->bvyz")
-    n_pw = lax.axis_size("pw")
-    width = planes * 2 * planes * grid
-    payload = piece.reshape(bands_here, n_pw, width).transpose(1, 0, 2)
-    payload = payload.reshape(n_pw, bands_here * width)
-    extra = jnp.broadcast_to(rows.reshape(1, -1), (n_pw, rows.size))
-    payload = jnp.concatenate([payload, extra], axis=1)
-    payload = lax.all_to_all(payload, "pw", split_axis=0, concat_axis=0, tiled=True)
-    gram = jnp.sum(payload[:, bands_here * width :], axis=0).reshape(rows.shape)
-    gram = gram / (columns * n_pw)
-    back = payload[:, : bands_here * width].reshape(n_pw, bands_here, planes, 2, planes, grid)
-    back = jnp.transpose(back, (1, 2, 3, 0, 4, 5))
+    piece = piece.reshape(bands_here, n_hi, n_lo, planes, 2, planes, grid)
+    piece, rows = exchange_with_rows(jnp.transpose(piece, (2, 0, 1, 3, 4, 5, 6)), rows, "pw_lo")
+    piece, rows = exchange_with_rows(jnp.transpose(piece, (2, 0, 1, 3, 4, 5, 6)), rows, "pw_hi")
+    gram = rows / (columns * n_hi * n_lo)
+    back = jnp.transpose(piece, (2, 3, 4, 0, 1, 5, 6))
     back = back.reshape(bands_here, planes, 2 * grid, grid)
     back = contract(back, dft_table(grid, False, "ck", "nd"), "bxwz,wv->bxvz")
     back = back.reshape(bands_here, planes, grid, 2 * grid)
@@ -91,11 +105,15 @@
 
 
 def solution(mesh):
-    placed = (P(None, "band", "pw"), P("pw"), P(None, "pw", None))
+    n_band, n_pw = mesh.devices.shape
+    n_hi = 4 if n_pw % 4 == 0 else 1
+    fine = Mesh(mesh.devices.reshape(n_band, n_hi, n_pw // n_hi), ("band", "pw_hi", "pw_lo"))
+    pw = ("pw_hi", "pw_lo")
+    placed = (P(None, "band", pw), P(pw), P(None, pw, None))
     return jax.shard_map(
         local,
-        mesh=mesh,
+        mesh=fine,
         in_specs=placed,
-        out_specs=(P(None, "band", "pw"), P(None, "band", None)),
+        out_specs=(P(None, "band", pw), P(None, "band", None)),
         check_vma=False,
     )

time: 95.9 us -> 112 us (1.17)
  the two profiles are of different devices: /device:TPU:16 before, /device:TPU:2 now
where the time goes in v6:
time: 112 us; the launch traced here: 111 us
  starting transfers between devices  38.5 us (34%)
  waiting for transfers between devices  27.1 us (24%)
  blocking collectives  24.3 us (22%)
  local copies, waits for them, and re-layouts  14.8 us (13%)
  matrix products  3.44 us (3%)
  other arithmetic  2.33 us (2%)
    all_to_all x2, blocking collectives, exchange_with_rows(): flat = lax.all_to_all(flat, axis, split_axis=0, concat_axis=0, tiled=True)  24.3 us
    all_to_all x2, waiting for transfers between devices, exchange(): lax.all_to_all(blocks.reshape(n, -1), axis, split_axis=0, concat_axis=0,...  20.4 us
    all_to_all x1, starting transfers between devices, gram_rows(): lax.all_to_all(pieces, 'band', split_axis=2, concat_axis=1, tiled=True)  18.3 us
    all_to_all x2, starting transfers between devices, exchange(): lax.all_to_all(blocks.reshape(n, -1), axis, split_axis=0, concat_axis=0,...  13.4 us
    all_to_all x1, starting transfers between devices, gram_rows(): lax.all_to_all(partial, 'band', split_axis=2, concat_axis=0, tiled=True)  6.74 us
    all_to_all x1, waiting for transfers between devices, gram_rows(): lax.all_to_all(partial, 'band', split_axis=2, concat_axis=0, tiled=True)  5.11 us
    unnamed x18, local copies, waits for them, and re-layouts  5 us
    dot_general x6, matrix products, contract(): return jnp.einsum(form, values, table, precision=HIGHEST)  3.26 us
  transfers between devices with their start and end apart: 4, of which 4 were waited for; matrix products, arithmetic and copies ran while one was open for 4% of the time, Pallas kernels for 0%

profile of v6, /device:TPU:2, one launch (start us, length us, event | category | flops | bytes accessed | tf_op | source)
XLA Modules:
  0.0 111.4 jit_solution(7169362037658703688)
XLA Ops:
  0.6 0.8 reduce.6
  1.6 0.6 copy.56
  2.2 18.3 %all-to-all-start.2 = ((f32[2,1,32,108]{3,0,1,2:T(2,128)}), f32[2,1,32,108]{3,0,1,2:T(2,128)S(1)}, u32[]{:S(2)}, u32[]{:S(2)}) async-start(f32[2,1,32,108]{3,0,1,2:T(2,128)} %copy.56), calls=%async_computation.2 | async-start | bytes 65536 | tf_op jit(solution)/shard_map/all_to_all | solution.py:53
  20.9 0.4 copy-done.7
  21.9 0.8 copy-done.5
  22.7 0.7 fusion.6
  23.5 0.8 copy-done.4
  24.3 0.5 fusion.7
  24.9 1.2 %all_to_all.54 = f32[8,1,6912]{2,1,0:T(1,128)} reshape(f32[8,1,3,2,4,3,96]{6,5,4,3,2,0,1:T(4,128)S(1)} %copy.49) | data formatting | bytes 442368 | tf_op jit(solution)/shard_map/all_to_all | solution.py:33
  26.1 1.6 %all-to-all-done.2 = f32[2,1,32,108]{3,0,1,2:T(2,128)S(1)} async-done(((f32[2,1,32,108]{3,0,1,2:T(2,128)}), f32[2,1,32,108]{3,0,1,2:T(2,128)S(1)}, u32[]{:S(2)}, u32[]{:S(2)}) %all-to-all-start.2) | async-done | bytes 27680 | tf_op jit(solution)/shard_map/all_to_all | solution.py:53
  27.7 7.6 %all-to-all-start = ((f32[8,1,6912]{2,1,0:T(1,128)}), f32[8,1,6912]{2,1,0:T(1,128)S(1)}, u32[]{:S(2)}, u32[]{:S(2)}) async-start(f32[8,1,6912]{2,1,0:T(1,128)} %all_to_all.54), calls=%async_computation | async-start | bytes 442368 | tf_op jit(solution)/shard_map/all_to_all | solution.py:33
  35.6 0.6 copy.58
  36.2 10.3 %all-to-all-done = f32[8,1,6912]{2,1,0:T(1,128)S(1)} async-done(((f32[8,1,6912]{2,1,0:T(1,128)}), f32[8,1,6912]{2,1,0:T(1,128)S(1)}, u32[]{:S(2)}, u32[]{:S(2)}) %all-to-all-start) | async-done | bytes 221216 | tf_op jit(solution)/shard_map/all_to_all | solution.py:33
  46.5 6.7 %all-to-all-start.3 = ((f32[1,2,32,1,32]{4,1,3,0,2:T(2,128)}), f32[1,2,32,1,32]{4,1,3,0,2:T(2,128)S(1)}, u32[]{:S(2)}, u32[]{:S(2)}) async-start(f32[1,2,32,1,32]{4,1,3,0,2:T(2,128)} %copy.58), calls=%async_computation.3 | async-start | bytes 65536 | tf_op jit(solution)/shard_map/all_to_all | solution.py:60
  53.3 0.5 reduce.7
  54.2 1.2 %all_to_all.55 = f32[4,1,13824]{2,1,0:T(1,128)} reshape(f32[4,8,1,3,2,3,96]{6,5,4,3,1,0,2:T(4,128)S(1)} %copy.51) | data formatting | bytes 442368 | tf_op jit(solution)/shard_map/all_to_all | solution.py:33
  55.3 5.1 %all-to-all-done.3 = f32[1,2,32,1,32]{4,1,3,0,2:T(2,128)S(1)} async-done(((f32[1,2,32,1,32]{4,1,3,0,2:T(2,128)}), f32[1,2,32,1,32]{4,1,3,0,2:T(2,128)S(1)}, u32[]{:S(2)}, u32[]{:S(2)}) %all-to-all-start.3) | async-done | bytes 8224 | tf_op jit(solution)/shard_map/all_to_all | solution.py:60
  60.5 5.9 %all-to-all-start.1 = ((f32[4,1,13824]{2,1,0:T(1,128)}), f32[4,1,13824]{2,1,0:T(1,128)S(1)}, u32[]{:S(2)}, u32[]{:S(2)}) async-start(f32[4,1,13824]{2,1,0:T(1,128)} %all_to_all.55), calls=%async_computation.1 | async-start | bytes 442368 | tf_op jit(solution)/shard_map/all_to_all | solution.py:33
  66.5 10.1 %all-to-all-done.1 = f32[4,1,13824]{2,1,0:T(1,128)S(1)} async-done(((f32[4,1,13824]{2,1,0:T(1,128)}), f32[4,1,13824]{2,1,0:T(1,128)S(1)}, u32[]{:S(2)}, u32[]{:S(2)}) %all-to-all-start.1) | async-done | bytes 221216 | tf_op jit(solution)/shard_map/all_to_all | solution.py:33
  76.5 0.6 reduce.8
  77.6 0.5 copy-done.1
  78.2 0.5 convolution_multiply_fusion
  78.9 0.7 copy-done.3
  79.6 0.5 convolution_bitcast_fusion.1
  80.8 12.5 %all_to_all.62 = f32[8,1,6976]{2,1,0:T(1,128)S(1)} all-to-all(f32[8,1,6976]{2,1,0:T(1,128)S(1)} %copy.59), channel_id=1, replica_groups=mesh['band'=32,'pw_hi'=4,'pw_lo'=8] {'pw_lo'}, dimensions={0} | all-to-all | bytes 446464 | tf_op jit(solution)/shard_map/all_to_all | solution.py:43
  94.4 11.8 %all_to_all.63 = f32[4,1,13888]{2,1,0:T(1,128)S(1)} all-to-all(f32[4,1,13888]{2,1,0:T(1,128)S(1)} %copy.61), channel_id=1, replica_groups=mesh['band'=32,'pw_hi'=4,'pw_lo'=8] {'pw_hi'}, dimensions={0} | all-to-all | bytes 444416 | tf_op jit(solution)/shard_map/all_to_all | solution.py:43
  106.3 0.6 div.10
  107.6 0.8 copy-done.2
  108.4 0.5 convolution_bitcast_fusion
  109.0 0.8 copy-done
  109.8 0.6 fusion
  110.6 0.9 reshape.171
  (53 shorter events, 5.5 us)
Async XLA Ops:
  2.2 25.5 %all-to-all-start.2 = ((f32[2,1,32,108]{3,0,1,2:T(2,128)}), f32[2,1,32,108]{3,0,1,2:T(2,128)S(1)}, u32[]{:S(2)}, u32[]{:S(2)}) async-start(f32[2,1,32,108]{3,0,1,2:T(2,128)} %copy.56), calls=%async_computation.2 | async-start | bytes 65536 | tf_op jit(solution)/shard_map/all_to_all | solution.py:53
  20.5 0.7 copy-start.7
  21.7 0.9 copy-start.5
  23.4 0.9 copy-start.4
  27.7 18.8 %all-to-all-start = ((f32[8,1,6912]{2,1,0:T(1,128)}), f32[8,1,6912]{2,1,0:T(1,128)S(1)}, u32[]{:S(2)}, u32[]{:S(2)}) async-start(f32[8,1,6912]{2,1,0:T(1,128)} %all_to_all.54), calls=%async_computation | async-start | bytes 442368 | tf_op jit(solution)/shard_map/all_to_all | solution.py:33
  46.5 13.9 %all-to-all-start.3 = ((f32[1,2,32,1,32]{4,1,3,0,2:T(2,128)}), f32[1,2,32,1,32]{4,1,3,0,2:T(2,128)S(1)}, u32[]{:S(2)}, u32[]{:S(2)}) async-start(f32[1,2,32,1,32]{4,1,3,0,2:T(2,128)} %copy.58), calls=%async_computation.3 | async-start | bytes 65536 | tf_op jit(solution)/shard_map/all_to_all | solution.py:60
  60.5 16.1 %all-to-all-start.1 = ((f32[4,1,13824]{2,1,0:T(1,128)}), f32[4,1,13824]{2,1,0:T(1,128)S(1)}, u32[]{:S(2)}, u32[]{:S(2)}) async-start(f32[4,1,13824]{2,1,0:T(1,128)} %all_to_all.55), calls=%async_computation.1 | async-start | bytes 442368 | tf_op jit(solution)/shard_map/all_to_all | solution.py:33
  77.2 0.9 copy-start.1
  77.2 1.0 copy-start.6
  78.7 0.9 copy-start.3
  107.4 0.9 copy-start.2
  108.9 1.0 copy-start

commit v7 on v2

--- a/solution.py
+++ b/solution.py
@@ -21,7 +21,7 @@
     perm_in = (0, 1) if rows == "ck" else (1, 0)
     perm_out = (2, 3) if cols == "dn" else (3, 2)
     table = np.transpose(table, perm_in + perm_out)
-    return jnp.asarray(table.reshape(2 * length, 2 * length).astype(np.float32))
+    return table.reshape(2 * length, 2 * length).astype(np.float32)
 
 
 def contract(values, table, form):
@@ -53,22 +53,26 @@
     lanes = lax.iota(jnp.int32, 8)
     hit = offsets[..., None] == lanes
     rows = gram_rows(orbitals)
+    kinds = [(True, "ck", "dn"), (True, "kc", "dn"), (True, "kc", "nd"),
+             (False, "kc", "nd"), (False, "ck", "nd"), (False, "ck", "dn")]
+    tables = jnp.asarray(np.stack([dft_table(grid, *kind) for kind in kinds]))
+    tables = lax.optimization_barrier(tables)
 
     coeffs = orbitals.reshape(2, bands_here, planes, grid, blocks)
     coeffs = jnp.transpose(coeffs, (1, 2, 3, 0, 4))
     spread = jnp.where(hit[None, :, :, None], coeffs[..., None], 0.0)
     spread = spread.reshape(bands_here, planes, grid, 2 * grid)
 
-    slab = contract(spread, dft_table(grid, True, "ck", "dn"), "bxyw,wv->bxyv")
+    slab = contract(spread, tables[0], "bxyw,wv->bxyv")
     slab = slab.reshape(bands_here, planes, 2 * grid, grid)
-    slab = contract(slab, dft_table(grid, True, "kc", "dn"), "bxwz,wv->bxvz")
+    slab = contract(slab, tables[1], "bxwz,wv->bxvz")
     slab = slab.reshape(bands_here, planes, 2, grid, grid)
     piece = lax.all_to_all(slab, "pw", split_axis=3, concat_axis=1, tiled=True)
     piece = piece.reshape(bands_here, 2 * grid, planes, grid)
-    piece = contract(piece, dft_table(grid, True, "kc", "nd"), "bwyz,wv->bvyz")
+    piece = contract(piece, tables[2], "bwyz,wv->bvyz")
     piece = piece.reshape(bands_here, grid, 2, planes, grid) * potential[None, :, None]
     piece = piece.reshape(bands_here, 2 * grid, planes, grid)
-    piece = contract(piece, dft_table(grid, False, "kc", "nd"), "bwyz,wv->bvyz")
+    piece = contract(piece, tables[3], "bwyz,wv->bvyz")
     n_pw = lax.axis_size("pw")
     width = planes * 2 * planes * grid
     payload = piece.reshape(bands_here, n_pw, width).transpose(1, 0, 2)
@@ -81,9 +85,9 @@
     back = payload[:, : bands_here * width].reshape(n_pw, bands_here, planes, 2, planes, grid)
     back = jnp.transpose(back, (1, 2, 3, 0, 4, 5))
     back = back.reshape(bands_here, planes, 2 * grid, grid)
-    back = contract(back, dft_table(grid, False, "ck", "nd"), "bxwz,wv->bxvz")
+    back = contract(back, tables[4], "bxwz,wv->bxvz")
     back = back.reshape(bands_here, planes, grid, 2 * grid)
-    back = contract(back, dft_table(grid, False, "ck", "dn"), "bxyw,wv->bxyv")
+    back = contract(back, tables[5], "bxyw,wv->bxyv")
     back = back.reshape(bands_here, planes, grid, 2, blocks, 8)
     picked = jnp.sum(jnp.where(hit[None, :, :, None], back, 0.0), axis=-1)
     applied = jnp.transpose(picked, (3, 0, 1, 2, 4)).reshape(2, bands_here, columns)

time: 95.9 us -> 94.2 us (0.982)
  blocking collectives: 18 us -> 0 us
  waiting for transfers between devices: 26.9 us -> 40.3 us
  starting transfers between devices: 33.9 us -> 38.7 us
  local copies, waits for them, and re-layouts: 11 us -> 7.82 us
    all_to_all x1 -> x0, blocking collectives: 18 us -> none  [local(): lax.all_to_all(payload, 'pw', split_axis=0, concat_axis=0, tiled=True)]
    all_to_all x0 -> x1, waiting for transfers between devices: none -> 13.3 us  [local(): lax.all_to_all(payload, 'pw', split_axis=0, concat_axis=0, tiled=True)]
    all_to_all x0 -> x1, starting transfers between devices: none -> 4.69 us  [local(): lax.all_to_all(payload, 'pw', split_axis=0, concat_axis=0, tiled=True)]
    unnamed x17 -> x5, local copies, waits for them, and re-layouts: 4.39 us -> 0.03 us
  transfers between devices with their start and end apart: 3 -> 4, of which waited for: 3 -> 4; matrix products, arithmetic and copies ran while one was open for 4% -> 5% of each run, Pallas kernels for 0% -> 0%
where the time goes in v7:
time: 94.2 us; the launch traced here: 93.7 us
  waiting for transfers between devices  40.3 us (43%)
  starting transfers between devices  38.7 us (41%)
  local copies, waits for them, and re-layouts  7.82 us (8%)
  matrix products  4.03 us (4%)
  other arithmetic  1.89 us (2%)
    all_to_all x1, starting transfers between devices, gram_rows(): lax.all_to_all(pieces, 'band', split_axis=2, concat_axis=1, tiled=True)  18.1 us
    all_to_all x1, waiting for transfers between devices, local(): piece = lax.all_to_all(slab, 'pw', split_axis=3, concat_axis=1, tiled=True)  14.2 us
    all_to_all x1, waiting for transfers between devices, local(): lax.all_to_all(payload, 'pw', split_axis=0, concat_axis=0, tiled=True)  13.3 us
    all_to_all x1, starting transfers between devices, local(): piece = lax.all_to_all(slab, 'pw', split_axis=3, concat_axis=1, tiled=True)  12.1 us
    all_to_all x1, waiting for transfers between devices, gram_rows(): lax.all_to_all(partial, 'band', split_axis=2, concat_axis=0, tiled=True)  6.83 us
    all_to_all x1, waiting for transfers between devices, gram_rows(): lax.all_to_all(pieces, 'band', split_axis=2, concat_axis=1, tiled=True)  5.92 us
    all_to_all x1, starting transfers between devices, local(): lax.all_to_all(payload, 'pw', split_axis=0, concat_axis=0, tiled=True)  4.69 us
    all_to_all x1, starting transfers between devices, gram_rows(): lax.all_to_all(partial, 'band', split_axis=2, concat_axis=0, tiled=True)  3.85 us
  transfers between devices with their start and end apart: 4, of which 4 were waited for; matrix products, arithmetic and copies ran while one was open for 5% of the time, Pallas kernels for 0%

profile of v7, /device:TPU:16, one launch (start us, length us, event | category | flops | bytes accessed | tf_op | source)
XLA Modules:
  0.0 93.7 jit_solution(7335705663040407463)
XLA Ops:
  0.6 0.8 reduce.6
  1.6 0.6 copy.67
  2.2 18.1 %all-to-all-start.1 = ((f32[2,1,32,108]{3,0,1,2:T(2,128)}), f32[2,1,32,108]{3,0,1,2:T(2,128)S(1)}, u32[]{:S(2)}, u32[]{:S(2)}) async-start(f32[2,1,32,108]{3,0,1,2:T(2,128)} %copy.67), calls=%async_computation.1 | async-start | bytes 65536 | tf_op jit(solution)/shard_map/all_to_all | solution.py:36
  20.4 0.3 reshape.121
  20.7 0.7 multiply_subtract_fusion
  21.4 0.2 eq.19
  21.7 0.1 copy.56
  22.0 0.7 fusion.4
  22.9 5.9 %all-to-all-done.1 = f32[2,1,32,108]{3,0,1,2:T(2,128)S(1)} async-done(((f32[2,1,32,108]{3,0,1,2:T(2,128)}), f32[2,1,32,108]{3,0,1,2:T(2,128)S(1)}, u32[]{:S(2)}, u32[]{:S(2)}) %all-to-all-start.1) | async-done | bytes 27680 | tf_op jit(solution)/shard_map/all_to_all | solution.py:36
  28.8 0.2 fusion.10
  29.1 0.6 copy.69
  29.7 3.8 %all-to-all-start.2 = ((f32[1,2,32,1,32]{4,1,3,0,2:T(2,128)}), f32[1,2,32,1,32]{4,1,3,0,2:T(2,128)S(1)}, u32[]{:S(2)}, u32[]{:S(2)}) async-start(f32[1,2,32,1,32]{4,1,3,0,2:T(2,128)} %copy.69), calls=%async_computation.2 | async-start | bytes 65536 | tf_op jit(solution)/shard_map/all_to_all | solution.py:43
  33.6 0.7 fusion.5
  34.3 0.9 %copy.60 = f32[1,3,2,96,96]{4,2,1,0,3:T(2,128)} copy(f32[1,3,2,96,96]{4,3,2,1,0:T(8,128)S(1)} %bitcast.88) | data formatting | bytes 442368 | tf_op jit(solution)/shard_map/reshape | solution.py:69
  35.2 6.8 %all-to-all-done.2 = f32[1,2,32,1,32]{4,1,3,0,2:T(2,128)S(1)} async-done(((f32[1,2,32,1,32]{4,1,3,0,2:T(2,128)}), f32[1,2,32,1,32]{4,1,3,0,2:T(2,128)S(1)}, u32[]{:S(2)}, u32[]{:S(2)}) %all-to-all-start.2) | async-done | bytes 8224 | tf_op jit(solution)/shard_map/all_to_all | solution.py:43
  42.0 12.1 %all-to-all-start = ((f32[1,3,2,96,96]{4,2,1,0,3:T(2,128)}), f32[1,3,2,96,96]{4,2,1,0,3:T(2,128)S(1)}, u32[]{:S(2)}, u32[]{:S(2)}) async-start(f32[1,3,2,96,96]{4,2,1,0,3:T(2,128)} %copy.60), calls=%async_computation | async-start | bytes 589824 | tf_op jit(solution)/shard_map/all_to_all | solution.py:70
  54.6 14.2 %all-to-all-done = f32[1,3,2,96,96]{4,2,1,0,3:T(2,128)S(1)} async-done(((f32[1,3,2,96,96]{4,2,1,0,3:T(2,128)}), f32[1,3,2,96,96]{4,2,1,0,3:T(2,128)S(1)}, u32[]{:S(2)}, u32[]{:S(2)}) %all-to-all-start) | async-done | bytes 221216 | tf_op jit(solution)/shard_map/all_to_all | solution.py:70
  69.1 0.5 convolution_multiply_fusion
  69.6 0.2 copy.64
  69.8 0.7 fusion.6
  70.5 0.2 copy.66
  70.7 0.2 transpose.33
  70.9 0.9 copy.70
  71.8 4.7 %all-to-all-start.3 = ((f32[32,1,1792]{2,1,0:T(1,128)}), f32[32,1,1792]{2,1,0:T(1,128)S(1)}, u32[]{:S(2)}, u32[]{:S(2)}) async-start(f32[32,1,1792]{2,1,0:T(1,128)} %copy.70), calls=%async_computation.3 | async-start | bytes 458752 | tf_op jit(solution)/shard_map/all_to_all | solution.py:82
  76.6 13.3 %all-to-all-done.3 = f32[32,1,1792]{2,1,0:T(1,128)S(1)} async-done(((f32[32,1,1792]{2,1,0:T(1,128)}), f32[32,1,1792]{2,1,0:T(1,128)S(1)}, u32[]{:S(2)}, u32[]{:S(2)}) %all-to-all-start.3) | async-done | bytes 229408 | tf_op jit(solution)/shard_map/all_to_all | solution.py:82
  90.1 0.6 div.10
  90.7 0.3 reshape.129
  91.1 0.1 reshape.130
  91.3 0.7 convolution_bitcast_fusion
  92.1 0.6 fusion
  92.7 0.1 copy.75
  92.9 0.9 reshape.142
  (28 shorter events, 1.7 us)
Async XLA Ops:
  2.2 19.8 %copy-start = (f32[6,192,192]{2,1,0:T(8,128)S(1)}, f32[6,192,192]{2,1,0:T(8,128)}, u32[]{:S(2)}) copy-start(f32[6,192,192]{2,1,0:T(8,128)} %constant.9.clone) | copy-start | bytes 2654212
  2.2 26.6 %all-to-all-start.1 = ((f32[2,1,32,108]{3,0,1,2:T(2,128)}), f32[2,1,32,108]{3,0,1,2:T(2,128)S(1)}, u32[]{:S(2)}, u32[]{:S(2)}) async-start(f32[2,1,32,108]{3,0,1,2:T(2,128)} %copy.67), calls=%async_computation.1 | async-start | bytes 65536 | tf_op jit(solution)/shard_map/all_to_all | solution.py:36
  29.7 12.3 %all-to-all-start.2 = ((f32[1,2,32,1,32]{4,1,3,0,2:T(2,128)}), f32[1,2,32,1,32]{4,1,3,0,2:T(2,128)S(1)}, u32[]{:S(2)}, u32[]{:S(2)}) async-start(f32[1,2,32,1,32]{4,1,3,0,2:T(2,128)} %copy.69), calls=%async_computation.2 | async-start | bytes 65536 | tf_op jit(solution)/shard_map/all_to_all | solution.py:43
  42.0 26.8 %all-to-all-start = ((f32[1,3,2,96,96]{4,2,1,0,3:T(2,128)}), f32[1,3,2,96,96]{4,2,1,0,3:T(2,128)S(1)}, u32[]{:S(2)}, u32[]{:S(2)}) async-start(f32[1,3,2,96,96]{4,2,1,0,3:T(2,128)} %copy.60), calls=%async_computation | async-start | bytes 589824 | tf_op jit(solution)/shard_map/all_to_all | solution.py:70
  54.1 14.9 %copy-start.1 = (f32[96,3,96]{2,0,1:T(8,128)S(1)}, f32[96,3,96]{2,0,1:T(8,128)}, u32[]{:S(2)}) copy-start(f32[96,3,96]{2,0,1:T(8,128)} %param.6) | copy-start | bytes 331780
  71.8 18.1 %all-to-all-start.3 = ((f32[32,1,1792]{2,1,0:T(1,128)}), f32[32,1,1792]{2,1,0:T(1,128)S(1)}, u32[]{:S(2)}, u32[]{:S(2)}) async-start(f32[32,1,1792]{2,1,0:T(1,128)} %copy.70), calls=%async_computation.3 | async-start | bytes 458752 | tf_op jit(solution)/shard_map/all_to_all | solution.py:82

commit v8 on v7

--- a/solution.py
+++ b/solution.py
@@ -32,16 +32,17 @@
     _, bands_here, columns = orbitals.shape
     n_band = lax.axis_size("band")
     chunk = columns // n_band
-    pieces = orbitals.reshape(2, bands_here, n_band, chunk)
-    pieces = lax.all_to_all(pieces, "band", split_axis=2, concat_axis=1, tiled=True)
+    pieces = lax.all_to_all(orbitals, "band", split_axis=2, concat_axis=2, tiled=True)
+    pieces = jnp.transpose(pieces.reshape(2, bands_here, n_band, chunk), (0, 2, 1, 3))
     bands = bands_here * n_band
     stacked = pieces.reshape(2 * bands, chunk)
     prod = lax.dot_general(stacked, stacked, (((1,), (1,)), ((), ())), precision=HIGHEST)
     gram_real = prod[:bands, :bands] + prod[bands:, bands:]
     gram_imag = prod[:bands, bands:] - prod[bands:, :bands]
-    partial = jnp.stack([gram_real, gram_imag]).reshape(1, 2, n_band, bands_here, bands)
-    rows = lax.all_to_all(partial, "band", split_axis=2, concat_axis=0, tiled=True)
-    return jnp.sum(rows, axis=0).reshape(2, bands_here, bands)
+    partial = jnp.stack([gram_real, gram_imag])
+    rows = lax.all_to_all(partial, "band", split_axis=1, concat_axis=1, tiled=True)
+    rows = rows.reshape(2, n_band, bands_here, bands)
+    return jnp.sum(rows, axis=1)
 
 
 def local(orbitals, pw_index, potential):

time: 94.2 us -> 118 us (1.25)
  other arithmetic: 1.89 us -> 16.5 us
  local copies, waits for them, and re-layouts: 7.82 us -> 16.9 us
    unnamed x1 -> x2, other arithmetic: 0.83 us -> 15.4 us
    unnamed x5 -> x13, local copies, waits for them, and re-layouts: 0.03 us -> 8.05 us
    all_to_all x1, local copies, waits for them, and re-layouts: 0.01 us -> 1.66 us  [gram_rows(): lax.all_to_all(orbitals, 'band', split_axis=2, concat_axis=2, tiled=True)]
    reshape x3 -> x0, local copies, waits for them, and re-layouts: 1.4 us -> none  [the longest x2 0.76 us: gram_rows(): pieces = orbitals.reshape(2, bands_here, n_band, chunk)]
  transfers between devices with their start and end apart: 4 -> 4, of which waited for: 4 -> 4; matrix products, arithmetic and copies ran while one was open for 5% -> 3% of each run, Pallas kernels for 0% -> 0%
where the time goes in v8:
time: 118 us
  waiting for transfers between devices  40.6 us (34%)
  starting transfers between devices  38.7 us (33%)
  local copies, waits for them, and re-layouts  16.9 us (14%)
  other arithmetic  16.5 us (14%)
  matrix products  4.02 us (3%)
    all_to_all x1, starting transfers between devices, gram_rows(): lax.all_to_all(orbitals, 'band', split_axis=2, concat_axis=2, tiled=True)  18 us
    unnamed x2, other arithmetic  15.4 us
    all_to_all x1, waiting for transfers between devices, local(): piece = lax.all_to_all(slab, 'pw', split_axis=3, concat_axis=1, tiled=True)  14.2 us
    all_to_all x1, waiting for transfers between devices, local(): lax.all_to_all(payload, 'pw', split_axis=0, concat_axis=0, tiled=True)  13.2 us
    all_to_all x1, starting transfers between devices, local(): piece = lax.all_to_all(slab, 'pw', split_axis=3, concat_axis=1, tiled=True)  12.1 us
    unnamed x13, local copies, waits for them, and re-layouts  8.05 us
    all_to_all x1, waiting for transfers between devices, gram_rows(): lax.all_to_all(partial, 'band', split_axis=1, concat_axis=1, tiled=True)  6.83 us
    all_to_all x1, waiting for transfers between devices, gram_rows(): lax.all_to_all(orbitals, 'band', split_axis=2, concat_axis=2, tiled=True)  6.3 us
  transfers between devices with their start and end apart: 4, of which 4 were waited for; matrix products, arithmetic and copies ran while one was open for 3% of the time, Pallas kernels for 0%

profile of v8, /device:TPU:16, one launch (start us, length us, event | category | flops | bytes accessed | tf_op | source)
XLA Modules:
  0.0 117.6 jit_solution(16038905143289610951)
XLA Ops:
  0.6 3.3 %copy.92 = f32[2,1,3456]{0,1,2:T(1,128)S(1)} copy(f32[2,1,3456]{2,1,0:T(1,128)} %param.4) | data formatting | bytes 55296 | tf_op args[0]
  4.0 0.5 broadcast.48
  4.5 15.3 %reduce.5 = f32[3456,2]{1,0:T(8,128)S(1)} reduce(f32[3456,1,2]{2,1,0:T(1,128)S(1)} %bitcast.88, f32[]{:T(128)} %broadcast.48), dimensions={1}, to_apply=%bitcast.76.reduce_sub_computation | reduce | bytes 55300
  19.8 1.4 %reshape.131 = f32[32,1,216]{2,1,0:T(1,128)} reshape(f32[3456,2]{1,0:T(8,128)S(1)} %reduce.5) | data formatting | bytes 55296
  21.3 18.0 %all-to-all-start.1 = ((f32[32,1,216]{2,1,0:T(1,128)}), f32[32,1,216]{2,1,0:T(1,128)S(1)}, u32[]{:S(2)}, u32[]{:S(2)}) async-start(f32[32,1,216]{2,1,0:T(1,128)} %reshape.131), calls=%async_computation.1 | async-start | bytes 65536 | tf_op jit(solution)/shard_map/all_to_all | solution.py:35
  39.7 0.3 reshape.110
  40.3 0.2 copy-done
  40.5 0.7 fusion.4
  41.4 6.3 %all-to-all-done.1 = f32[32,1,216]{2,1,0:T(1,128)S(1)} async-done(((f32[32,1,216]{2,1,0:T(1,128)}), f32[32,1,216]{2,1,0:T(1,128)S(1)}, u32[]{:S(2)}, u32[]{:S(2)}) %all-to-all-start.1) | async-done | bytes 27680 | tf_op jit(solution)/shard_map/all_to_all | solution.py:35
  47.7 0.7 reduce.6
  48.4 2.5 %reshape.132 = f32[3456,1,2]{2,1,0:T(1,128)S(1)} reshape(f32[32,216]{1,0:T(8,128)S(1)} %reduce.6) | data formatting | bytes 55296
  50.9 1.7 %copy.93 = f32[2,1,3456]{2,0,1:T(2,128)S(1)} copy(f32[2,1,3456]{0,1,2:T(1,128)S(1)} %bitcast.87) | data formatting | bytes 55296 | tf_op jit(solution)/shard_map/all_to_all | solution.py:35
  53.0 0.6 copy.94
  53.7 3.8 %all-to-all-start.2 = ((f32[2,32,32]{2,0,1:T(2,128)}), f32[2,32,32]{2,0,1:T(2,128)S(1)}, u32[]{:S(2)}, u32[]{:S(2)}) async-start(f32[2,32,32]{2,0,1:T(2,128)} %copy.94), calls=%async_computation.2 | async-start | bytes 65536 | tf_op jit(solution)/shard_map/all_to_all | solution.py:43
  57.5 0.7 fusion.5
  58.2 0.9 copy.85
  59.1 6.8 %all-to-all-done.2 = f32[2,32,32]{2,0,1:T(2,128)S(1)} async-done(((f32[2,32,32]{2,0,1:T(2,128)}), f32[2,32,32]{2,0,1:T(2,128)S(1)}, u32[]{:S(2)}, u32[]{:S(2)}) %all-to-all-start.2) | async-done | bytes 8224 | tf_op jit(solution)/shard_map/all_to_all | solution.py:43
  65.9 12.1 %all-to-all-start = ((f32[1,3,2,96,96]{4,2,1,0,3:T(2,128)}), f32[1,3,2,96,96]{4,2,1,0,3:T(2,128)S(1)}, u32[]{:S(2)}, u32[]{:S(2)}) async-start(f32[1,3,2,96,96]{4,2,1,0,3:T(2,128)} %copy.85), calls=%async_computation | async-start | bytes 589824 | tf_op jit(solution)/shard_map/all_to_all | solution.py:71
  78.5 14.2 %all-to-all-done = f32[1,3,2,96,96]{4,2,1,0,3:T(2,128)S(1)} async-done(((f32[1,3,2,96,96]{4,2,1,0,3:T(2,128)}), f32[1,3,2,96,96]{4,2,1,0,3:T(2,128)S(1)}, u32[]{:S(2)}, u32[]{:S(2)}) %all-to-all-start) | async-done | bytes 221216 | tf_op jit(solution)/shard_map/all_to_all | solution.py:71
  92.9 0.5 convolution_multiply_fusion
  93.4 0.2 copy.89
  93.6 0.7 fusion.6
  94.3 0.2 copy.91
  94.5 0.2 transpose.33
  94.8 0.9 copy.95
  95.7 4.8 %all-to-all-start.3 = ((f32[32,1,1792]{2,1,0:T(1,128)}), f32[32,1,1792]{2,1,0:T(1,128)S(1)}, u32[]{:S(2)}, u32[]{:S(2)}) async-start(f32[32,1,1792]{2,1,0:T(1,128)} %copy.95), calls=%async_computation.3 | async-start | bytes 458752 | tf_op jit(solution)/shard_map/all_to_all | solution.py:83
  100.6 13.2 %all-to-all-done.3 = f32[32,1,1792]{2,1,0:T(1,128)S(1)} async-done(((f32[32,1,1792]{2,1,0:T(1,128)}), f32[32,1,1792]{2,1,0:T(1,128)S(1)}, u32[]{:S(2)}, u32[]{:S(2)}) %all-to-all-start.3) | async-done | bytes 229408 | tf_op jit(solution)/shard_map/all_to_all | solution.py:83
  114.0 0.6 div.10
  114.6 0.3 reshape.115
  115.2 0.7 convolution_bitcast_fusion
  115.9 0.6 fusion
  116.7 0.9 reshape.128
  (37 shorter events, 2.5 us)
Async XLA Ops:
  19.8 19.4 %copy-start.2 = (f32[2,1,3456]{2,1,0:T(1,128)S(1)}, f32[2,1,3456]{2,1,0:T(1,128)}, u32[]{:S(2)}) copy-start(f32[2,1,3456]{2,1,0:T(1,128)} %param.4) | copy-start | bytes 82948
  19.8 19.5 %copy-start.3 = (s32[3456]{0:T(1024)S(1)}, s32[3456]{0:T(1024)}, u32[]{:S(2)}) copy-start(s32[3456]{0:T(1024)} %param.5) | copy-start | bytes 41476
  21.3 26.4 %all-to-all-start.1 = ((f32[32,1,216]{2,1,0:T(1,128)}), f32[32,1,216]{2,1,0:T(1,128)S(1)}, u32[]{:S(2)}, u32[]{:S(2)}) async-start(f32[32,1,216]{2,1,0:T(1,128)} %reshape.131), calls=%async_computation.1 | async-start | bytes 65536 | tf_op jit(solution)/shard_map/all_to_all | solution.py:35
  39.3 1.3 %copy-start = (f32[6,192,192]{2,1,0:T(8,128)S(1)}, f32[6,192,192]{2,1,0:T(8,128)}, u32[]{:S(2)}) copy-start(f32[6,192,192]{2,1,0:T(8,128)} %constant.9.clone) | copy-start | bytes 2654212
  53.7 12.3 %all-to-all-start.2 = ((f32[2,32,32]{2,0,1:T(2,128)}), f32[2,32,32]{2,0,1:T(2,128)S(1)}, u32[]{:S(2)}, u32[]{:S(2)}) async-start(f32[2,32,32]{2,0,1:T(2,128)} %copy.94), calls=%async_computation.2 | async-start | bytes 65536 | tf_op jit(solution)/shard_map/all_to_all | solution.py:43
  65.9 26.8 %all-to-all-start = ((f32[1,3,2,96,96]{4,2,1,0,3:T(2,128)}), f32[1,3,2,96,96]{4,2,1,0,3:T(2,128)S(1)}, u32[]{:S(2)}, u32[]{:S(2)}) async-start(f32[1,3,2,96,96]{4,2,1,0,3:T(2,128)} %copy.85), calls=%async_computation | async-start | bytes 589824 | tf_op jit(solution)/shard_map/all_to_all | solution.py:71
  78.1 14.9 %copy-start.1 = (f32[96,3,96]{2,0,1:T(8,128)S(1)}, f32[96,3,96]{2,0,1:T(8,128)}, u32[]{:S(2)}) copy-start(f32[96,3,96]{2,0,1:T(8,128)} %param.6) | copy-start | bytes 331780
  95.7 18.2 %all-to-all-start.3 = ((f32[32,1,1792]{2,1,0:T(1,128)}), f32[32,1,1792]{2,1,0:T(1,128)S(1)}, u32[]{:S(2)}, u32[]{:S(2)}) async-start(f32[32,1,1792]{2,1,0:T(1,128)} %copy.95), calls=%async_computation.3 | async-start | bytes 458752 | tf_op jit(solution)/shard_map/all_to_all | solution.py:83

commit v9 on v7

--- a/solution.py
+++ b/solution.py
@@ -79,7 +79,11 @@
     payload = payload.reshape(n_pw, bands_here * width)
     extra = jnp.broadcast_to(rows.reshape(1, -1), (n_pw, rows.size))
     payload = jnp.concatenate([payload, extra], axis=1)
+    length = payload.shape[1]
+    if length % 128 == 0:
+        payload = payload.reshape(n_pw, length // 128, 128)
     payload = lax.all_to_all(payload, "pw", split_axis=0, concat_axis=0, tiled=True)
+    payload = payload.reshape(n_pw, length)
     gram = jnp.sum(payload[:, bands_here * width :], axis=0).reshape(rows.shape)
     gram = gram / (columns * n_pw)
     back = payload[:, : bands_here * width].reshape(n_pw, bands_here, planes, 2, planes, grid)

time: 94.2 us -> 94.7 us (level)
  no operation moved by 1% of the time
where the time goes in v9:
time: 94.7 us; the launch traced here: 94.2 us
  waiting for transfers between devices  41 us (43%)
  starting transfers between devices  38.7 us (41%)
  local copies, waits for them, and re-layouts  7.7 us (8%)
  matrix products  4.03 us (4%)
  other arithmetic  1.89 us (2%)
    all_to_all x1, starting transfers between devices, gram_rows(): lax.all_to_all(pieces, 'band', split_axis=2, concat_axis=1, tiled=True)  18.1 us
    all_to_all x1, waiting for transfers between devices, local(): piece = lax.all_to_all(slab, 'pw', split_axis=3, concat_axis=1, tiled=True)  14.2 us
    all_to_all x1, waiting for transfers between devices, local(): lax.all_to_all(payload, 'pw', split_axis=0, concat_axis=0, tiled=True)  14 us
    all_to_all x1, starting transfers between devices, local(): piece = lax.all_to_all(slab, 'pw', split_axis=3, concat_axis=1, tiled=True)  12.1 us
    all_to_all x1, waiting for transfers between devices, gram_rows(): lax.all_to_all(partial, 'band', split_axis=2, concat_axis=0, tiled=True)  6.83 us
    all_to_all x1, waiting for transfers between devices, gram_rows(): lax.all_to_all(pieces, 'band', split_axis=2, concat_axis=1, tiled=True)  5.92 us
    all_to_all x1, starting transfers between devices, local(): lax.all_to_all(payload, 'pw', split_axis=0, concat_axis=0, tiled=True)  4.69 us
    all_to_all x1, starting transfers between devices, gram_rows(): lax.all_to_all(partial, 'band', split_axis=2, concat_axis=0, tiled=True)  3.85 us
  transfers between devices with their start and end apart: 4, of which 4 were waited for; matrix products, arithmetic and copies ran while one was open for 5% of the time, Pallas kernels for 0%

profile of v9, /device:TPU:16, one launch (start us, length us, event | category | flops | bytes accessed | tf_op | source)
XLA Modules:
  0.0 94.2 jit_solution(17383657774001986645)
XLA Ops:
  0.6 0.8 reduce.6
  1.6 0.6 copy.66
  2.2 18.1 %all-to-all-start.1 = ((f32[2,1,32,108]{3,0,1,2:T(2,128)}), f32[2,1,32,108]{3,0,1,2:T(2,128)S(1)}, u32[]{:S(2)}, u32[]{:S(2)}) async-start(f32[2,1,32,108]{3,0,1,2:T(2,128)} %copy.66), calls=%async_computation.1 | async-start | bytes 65536 | tf_op jit(solution)/shard_map/all_to_all | solution.py:36
  20.4 0.3 reshape.125
  20.7 0.7 multiply_subtract_fusion
  21.4 0.2 eq.19
  21.7 0.1 copy.55
  22.0 0.7 fusion.4
  22.9 5.9 %all-to-all-done.1 = f32[2,1,32,108]{3,0,1,2:T(2,128)S(1)} async-done(((f32[2,1,32,108]{3,0,1,2:T(2,128)}), f32[2,1,32,108]{3,0,1,2:T(2,128)S(1)}, u32[]{:S(2)}, u32[]{:S(2)}) %all-to-all-start.1) | async-done | bytes 27680 | tf_op jit(solution)/shard_map/all_to_all | solution.py:36
  28.8 0.2 fusion.10
  29.1 0.6 copy.68
  29.7 3.8 %all-to-all-start.2 = ((f32[1,2,32,1,32]{4,1,3,0,2:T(2,128)}), f32[1,2,32,1,32]{4,1,3,0,2:T(2,128)S(1)}, u32[]{:S(2)}, u32[]{:S(2)}) async-start(f32[1,2,32,1,32]{4,1,3,0,2:T(2,128)} %copy.68), calls=%async_computation.2 | async-start | bytes 65536 | tf_op jit(solution)/shard_map/all_to_all | solution.py:43
  33.6 0.7 fusion.5
  34.3 0.9 copy.59
  35.2 6.8 %all-to-all-done.2 = f32[1,2,32,1,32]{4,1,3,0,2:T(2,128)S(1)} async-done(((f32[1,2,32,1,32]{4,1,3,0,2:T(2,128)}), f32[1,2,32,1,32]{4,1,3,0,2:T(2,128)S(1)}, u32[]{:S(2)}, u32[]{:S(2)}) %all-to-all-start.2) | async-done | bytes 8224 | tf_op jit(solution)/shard_map/all_to_all | solution.py:43
  42.0 12.1 %all-to-all-start = ((f32[1,3,2,96,96]{4,2,1,0,3:T(2,128)}), f32[1,3,2,96,96]{4,2,1,0,3:T(2,128)S(1)}, u32[]{:S(2)}, u32[]{:S(2)}) async-start(f32[1,3,2,96,96]{4,2,1,0,3:T(2,128)} %copy.59), calls=%async_computation | async-start | bytes 589824 | tf_op jit(solution)/shard_map/all_to_all | solution.py:70
  54.6 14.2 %all-to-all-done = f32[1,3,2,96,96]{4,2,1,0,3:T(2,128)S(1)} async-done(((f32[1,3,2,96,96]{4,2,1,0,3:T(2,128)}), f32[1,3,2,96,96]{4,2,1,0,3:T(2,128)S(1)}, u32[]{:S(2)}, u32[]{:S(2)}) %all-to-all-start) | async-done | bytes 221216 | tf_op jit(solution)/shard_map/all_to_all | solution.py:70
  69.1 0.5 convolution_multiply_fusion
  69.6 0.2 copy.63
  69.8 0.7 fusion.6
  70.5 0.2 copy.65
  70.7 0.2 transpose.33
  70.9 0.7 reshape.133
  71.7 4.7 %all-to-all-start.3 = ((f32[32,14,128]{2,1,0:T(8,128)}), f32[32,14,128]{2,1,0:T(8,128)S(1)}, u32[]{:S(2)}, u32[]{:S(2)}) async-start(f32[32,14,128]{2,1,0:T(8,128)} %reshape.133), calls=%async_computation.3 | async-start | bytes 524288 | tf_op jit(solution)/shard_map/all_to_all | solution.py:85
  76.5 14.0 %all-to-all-done.3 = f32[32,14,128]{2,1,0:T(8,128)S(1)} async-done(((f32[32,14,128]{2,1,0:T(8,128)}), f32[32,14,128]{2,1,0:T(8,128)S(1)}, u32[]{:S(2)}, u32[]{:S(2)}) %all-to-all-start.3) | async-done | bytes 229408 | tf_op jit(solution)/shard_map/all_to_all | solution.py:85
  90.6 0.6 div.10
  91.3 0.3 reshape.135
  91.7 0.1 reshape.136
  91.8 0.7 convolution_bitcast_fusion
  92.6 0.6 fusion
  93.2 0.1 copy.73
  93.4 0.9 reshape.148
  (28 shorter events, 1.7 us)
Async XLA Ops:
  2.2 19.8 %copy-start = (f32[6,192,192]{2,1,0:T(8,128)S(1)}, f32[6,192,192]{2,1,0:T(8,128)}, u32[]{:S(2)}) copy-start(f32[6,192,192]{2,1,0:T(8,128)} %constant.9.clone) | copy-start | bytes 2654212
  2.2 26.6 %all-to-all-start.1 = ((f32[2,1,32,108]{3,0,1,2:T(2,128)}), f32[2,1,32,108]{3,0,1,2:T(2,128)S(1)}, u32[]{:S(2)}, u32[]{:S(2)}) async-start(f32[2,1,32,108]{3,0,1,2:T(2,128)} %copy.66), calls=%async_computation.1 | async-start | bytes 65536 | tf_op jit(solution)/shard_map/all_to_all | solution.py:36
  29.7 12.3 %all-to-all-start.2 = ((f32[1,2,32,1,32]{4,1,3,0,2:T(2,128)}), f32[1,2,32,1,32]{4,1,3,0,2:T(2,128)S(1)}, u32[]{:S(2)}, u32[]{:S(2)}) async-start(f32[1,2,32,1,32]{4,1,3,0,2:T(2,128)} %copy.68), calls=%async_computation.2 | async-start | bytes 65536 | tf_op jit(solution)/shard_map/all_to_all | solution.py:43
  42.0 26.8 %all-to-all-start = ((f32[1,3,2,96,96]{4,2,1,0,3:T(2,128)}), f32[1,3,2,96,96]{4,2,1,0,3:T(2,128)S(1)}, u32[]{:S(2)}, u32[]{:S(2)}) async-start(f32[1,3,2,96,96]{4,2,1,0,3:T(2,128)} %copy.59), calls=%async_computation | async-start | bytes 589824 | tf_op jit(solution)/shard_map/all_to_all | solution.py:70
  54.1 14.9 %copy-start.1 = (f32[96,3,96]{2,0,1:T(8,128)S(1)}, f32[96,3,96]{2,0,1:T(8,128)}, u32[]{:S(2)}) copy-start(f32[96,3,96]{2,0,1:T(8,128)} %param.6) | copy-start | bytes 331780
  71.7 18.8 %all-to-all-start.3 = ((f32[32,14,128]{2,1,0:T(8,128)}), f32[32,14,128]{2,1,0:T(8,128)S(1)}, u32[]{:S(2)}, u32[]{:S(2)}) async-start(f32[32,14,128]{2,1,0:T(8,128)} %reshape.133), calls=%async_computation.3 | async-start | bytes 524288 | tf_op jit(solution)/shard_map/all_to_all | solution.py:85

commit v10 on v7

--- a/solution.py
+++ b/solution.py
@@ -39,7 +39,11 @@
     prod = lax.dot_general(stacked, stacked, (((1,), (1,)), ((), ())), precision=HIGHEST)
     gram_real = prod[:bands, :bands] + prod[bands:, bands:]
     gram_imag = prod[:bands, bands:] - prod[bands:, :bands]
-    partial = jnp.stack([gram_real, gram_imag]).reshape(1, 2, n_band, bands_here, bands)
+    return jnp.stack([gram_real, gram_imag]).reshape(1, 2, n_band, bands_here, bands)
+
+
+def scatter_rows(partial):
+    _, _, _, bands_here, bands = partial.shape
     rows = lax.all_to_all(partial, "band", split_axis=2, concat_axis=0, tiled=True)
     return jnp.sum(rows, axis=0).reshape(2, bands_here, bands)
 
@@ -52,7 +56,7 @@
     offsets = (pw_index - 8 * lax.iota(jnp.int32, columns)).reshape(planes, grid, blocks)
     lanes = lax.iota(jnp.int32, 8)
     hit = offsets[..., None] == lanes
-    rows = gram_rows(orbitals)
+    partial = gram_rows(orbitals)
     kinds = [(True, "ck", "dn"), (True, "kc", "dn"), (True, "kc", "nd"),
              (False, "kc", "nd"), (False, "ck", "nd"), (False, "ck", "dn")]
     tables = jnp.asarray(np.stack([dft_table(grid, *kind) for kind in kinds]))
@@ -68,6 +72,8 @@
     slab = contract(slab, tables[1], "bxwz,wv->bxvz")
     slab = slab.reshape(bands_here, planes, 2, grid, grid)
     piece = lax.all_to_all(slab, "pw", split_axis=3, concat_axis=1, tiled=True)
+    piece, partial = lax.optimization_barrier((piece, partial))
+    rows = scatter_rows(partial)
     piece = piece.reshape(bands_here, 2 * grid, planes, grid)
     piece = contract(piece, tables[2], "bwyz,wv->bvyz")
     piece = piece.reshape(bands_here, grid, 2, planes, grid) * potential[None, :, None]

time: 94.2 us -> 93.2 us (0.989)
  waiting for transfers between devices: 40.3 us -> 38.4 us
    all_to_all x1, waiting for transfers between devices: 5.92 us -> 4.05 us  [gram_rows(): lax.all_to_all(pieces, 'band', split_axis=2, concat_axis=1, tiled=True)]
  transfers between devices with their start and end apart: 4 -> 4, of which waited for: 4 -> 4; matrix products, arithmetic and copies ran while one was open for 5% -> 7% of each run, Pallas kernels for 0% -> 0%
where the time goes in v10:
time: 93.2 us; the launch traced here: 92.7 us
  starting transfers between devices  39.5 us (42%)
  waiting for transfers between devices  38.4 us (41%)
  local copies, waits for them, and re-layouts  7.88 us (8%)
  matrix products  4.03 us (4%)
  other arithmetic  1.89 us (2%)
    all_to_all x1, starting transfers between devices, gram_rows(): lax.all_to_all(pieces, 'band', split_axis=2, concat_axis=1, tiled=True)  18.1 us
    all_to_all x1, waiting for transfers between devices, local(): piece = lax.all_to_all(slab, 'pw', split_axis=3, concat_axis=1, tiled=True)  14.4 us
    all_to_all x1, waiting for transfers between devices, local(): lax.all_to_all(payload, 'pw', split_axis=0, concat_axis=0, tiled=True)  13.3 us
    all_to_all x1, starting transfers between devices, local(): piece = lax.all_to_all(slab, 'pw', split_axis=3, concat_axis=1, tiled=True)  12.1 us
    all_to_all x1, waiting for transfers between devices, scatter_rows(): lax.all_to_all(partial, 'band', split_axis=2, concat_axis=0, tiled=True)  6.6 us
    all_to_all x1, starting transfers between devices, local(): lax.all_to_all(payload, 'pw', split_axis=0, concat_axis=0, tiled=True)  4.73 us
    all_to_all x1, starting transfers between devices, scatter_rows(): lax.all_to_all(partial, 'band', split_axis=2, concat_axis=0, tiled=True)  4.62 us
    all_to_all x1, waiting for transfers between devices, gram_rows(): lax.all_to_all(pieces, 'band', split_axis=2, concat_axis=1, tiled=True)  4.05 us
  transfers between devices with their start and end apart: 4, of which 4 were waited for; matrix products, arithmetic and copies ran while one was open for 7% of the time, Pallas kernels for 0%

profile of v10, /device:TPU:16, one launch (start us, length us, event | category | flops | bytes accessed | tf_op | source)
XLA Modules:
  0.0 92.7 jit_solution(8169308657980176366)
XLA Ops:
  0.6 0.8 reduce.6
  1.6 0.6 copy.100
  2.2 18.1 %all-to-all-start.1 = ((f32[2,1,32,108]{3,0,1,2:T(2,128)}), f32[2,1,32,108]{3,0,1,2:T(2,128)S(1)}, u32[]{:S(2)}, u32[]{:S(2)}) async-start(f32[2,1,32,108]{3,0,1,2:T(2,128)} %copy.100), calls=%async_computation.1 | async-start | bytes 65536 | tf_op jit(solution)/shard_map/all_to_all | solution.py:36
  20.4 0.3 reshape.120
  20.7 0.7 multiply_subtract_fusion
  21.4 0.2 eq.19
  21.7 0.1 copy.93
  22.0 0.7 fusion.4
  22.9 0.7 fusion.5
  23.6 0.9 %copy.97 = f32[1,3,2,96,96]{4,2,1,0,3:T(2,128)} copy(f32[1,3,2,96,96]{4,3,2,1,0:T(8,128)S(1)} %bitcast.89) | data formatting | bytes 442368 | tf_op jit(solution)/shard_map/reshape | solution.py:73
  24.8 4.0 %all-to-all-done.1 = f32[2,1,32,108]{3,0,1,2:T(2,128)S(1)} async-done(((f32[2,1,32,108]{3,0,1,2:T(2,128)}), f32[2,1,32,108]{3,0,1,2:T(2,128)S(1)}, u32[]{:S(2)}, u32[]{:S(2)}) %all-to-all-start.1) | async-done | bytes 27680 | tf_op jit(solution)/shard_map/all_to_all | solution.py:36
  28.8 12.1 %all-to-all-start = ((f32[1,3,2,96,96]{4,2,1,0,3:T(2,128)}), f32[1,3,2,96,96]{4,2,1,0,3:T(2,128)S(1)}, u32[]{:S(2)}, u32[]{:S(2)}) async-start(f32[1,3,2,96,96]{4,2,1,0,3:T(2,128)} %copy.97), calls=%async_computation | async-start | bytes 589824 | tf_op jit(solution)/shard_map/all_to_all | solution.py:74
  40.9 0.2 fusion.10
  41.2 14.4 %all-to-all-done = f32[1,3,2,96,96]{4,2,1,0,3:T(2,128)S(1)} async-done(((f32[1,3,2,96,96]{4,2,1,0,3:T(2,128)}), f32[1,3,2,96,96]{4,2,1,0,3:T(2,128)S(1)}, u32[]{:S(2)}, u32[]{:S(2)}) %all-to-all-start) | async-done | bytes 221216 | tf_op jit(solution)/shard_map/all_to_all | solution.py:74
  55.9 0.6 copy.107
  56.6 4.6 %all-to-all-start.2 = ((f32[1,2,32,1,32]{4,1,3,0,2:T(2,128)}), f32[1,2,32,1,32]{4,1,3,0,2:T(2,128)S(1)}, u32[]{:S(2)}, u32[]{:S(2)}) async-start(f32[1,2,32,1,32]{4,1,3,0,2:T(2,128)} %copy.107), calls=%async_computation.2 | async-start | bytes 65536 | tf_op jit(solution)/shard_map/all_to_all | solution.py:47
  61.2 0.5 convolution_multiply_fusion
  61.7 0.2 copy.104
  61.9 0.7 fusion.6
  62.6 0.2 copy.106
  62.8 0.2 transpose.33
  63.0 6.6 %all-to-all-done.2 = f32[1,2,32,1,32]{4,1,3,0,2:T(2,128)S(1)} async-done(((f32[1,2,32,1,32]{4,1,3,0,2:T(2,128)}), f32[1,2,32,1,32]{4,1,3,0,2:T(2,128)S(1)}, u32[]{:S(2)}, u32[]{:S(2)}) %all-to-all-start.2) | async-done | bytes 8224 | tf_op jit(solution)/shard_map/all_to_all | solution.py:47
  69.8 0.9 copy.108
  70.8 4.7 %all-to-all-start.3 = ((f32[32,1,1792]{2,1,0:T(1,128)}), f32[32,1,1792]{2,1,0:T(1,128)S(1)}, u32[]{:S(2)}, u32[]{:S(2)}) async-start(f32[32,1,1792]{2,1,0:T(1,128)} %copy.108), calls=%async_computation.3 | async-start | bytes 458752 | tf_op jit(solution)/shard_map/all_to_all | solution.py:88
  75.6 13.3 %all-to-all-done.3 = f32[32,1,1792]{2,1,0:T(1,128)S(1)} async-done(((f32[32,1,1792]{2,1,0:T(1,128)}), f32[32,1,1792]{2,1,0:T(1,128)S(1)}, u32[]{:S(2)}, u32[]{:S(2)}) %all-to-all-start.3) | async-done | bytes 229408 | tf_op jit(solution)/shard_map/all_to_all | solution.py:88
  89.0 0.6 div.10
  89.7 0.3 reshape.128
  90.1 0.1 reshape.129
  90.2 0.7 convolution_bitcast_fusion
  91.0 0.6 fusion
  91.6 0.1 copy.113
  91.8 0.9 reshape.141
  (29 shorter events, 1.7 us)
Async XLA Ops:
  2.2 19.8 %copy-start = (f32[6,192,192]{2,1,0:T(8,128)S(1)}, f32[6,192,192]{2,1,0:T(8,128)}, u32[]{:S(2)}) copy-start(f32[6,192,192]{2,1,0:T(8,128)} %constant.9.clone) | copy-start | bytes 2654212
  2.2 26.6 %all-to-all-start.1 = ((f32[2,1,32,108]{3,0,1,2:T(2,128)}), f32[2,1,32,108]{3,0,1,2:T(2,128)S(1)}, u32[]{:S(2)}, u32[]{:S(2)}) async-start(f32[2,1,32,108]{3,0,1,2:T(2,128)} %copy.100), calls=%async_computation.1 | async-start | bytes 65536 | tf_op jit(solution)/shard_map/all_to_all | solution.py:36
  28.8 26.8 %all-to-all-start = ((f32[1,3,2,96,96]{4,2,1,0,3:T(2,128)}), f32[1,3,2,96,96]{4,2,1,0,3:T(2,128)S(1)}, u32[]{:S(2)}, u32[]{:S(2)}) async-start(f32[1,3,2,96,96]{4,2,1,0,3:T(2,128)} %copy.97), calls=%async_computation | async-start | bytes 589824 | tf_op jit(solution)/shard_map/all_to_all | solution.py:74
  40.9 20.3 %copy-start.1 = (f32[96,3,96]{2,0,1:T(8,128)S(1)}, f32[96,3,96]{2,0,1:T(8,128)}, u32[]{:S(2)}) copy-start(f32[96,3,96]{2,0,1:T(8,128)} %param.6) | copy-start | bytes 331780
  56.6 13.1 %all-to-all-start.2 = ((f32[1,2,32,1,32]{4,1,3,0,2:T(2,128)}), f32[1,2,32,1,32]{4,1,3,0,2:T(2,128)S(1)}, u32[]{:S(2)}, u32[]{:S(2)}) async-start(f32[1,2,32,1,32]{4,1,3,0,2:T(2,128)} %copy.107), calls=%async_computation.2 | async-start | bytes 65536 | tf_op jit(solution)/shard_map/all_to_all | solution.py:47
  70.8 18.2 %all-to-all-start.3 = ((f32[32,1,1792]{2,1,0:T(1,128)}), f32[32,1,1792]{2,1,0:T(1,128)S(1)}, u32[]{:S(2)}, u32[]{:S(2)}) async-start(f32[32,1,1792]{2,1,0:T(1,128)} %copy.108), calls=%async_computation.3 | async-start | bytes 458752 | tf_op jit(solution)/shard_map/all_to_all | solution.py:88

commit v11 on v10

--- a/solution.py
+++ b/solution.py
@@ -83,8 +83,10 @@
     width = planes * 2 * planes * grid
     payload = piece.reshape(bands_here, n_pw, width).transpose(1, 0, 2)
     payload = payload.reshape(n_pw, bands_here * width)
+    payload = jnp.concatenate([payload, jnp.zeros((n_pw, rows.size), payload.dtype)], axis=1)
+    payload = lax.optimization_barrier(payload)
     extra = jnp.broadcast_to(rows.reshape(1, -1), (n_pw, rows.size))
-    payload = jnp.concatenate([payload, extra], axis=1)
+    payload = lax.dynamic_update_slice(payload, extra, (0, bands_here * width))
     payload = lax.all_to_all(payload, "pw", split_axis=0, concat_axis=0, tiled=True)
     gram = jnp.sum(payload[:, bands_here * width :], axis=0).reshape(rows.shape)
     gram = gram / (columns * n_pw)

time: 93.2 us -> 93.4 us (level)
    dynamic_update_slice x0 -> x2, local copies, waits for them, and re-layouts: none -> 1.21 us  [local(): payload = lax.dynamic_update_slice(payload, extra, (0, bands_here * width))]
where the time goes in v11:
time: 93.4 us; the launch traced here: 92.9 us
  starting transfers between devices  39.5 us (42%)
  waiting for transfers between devices  38.4 us (41%)
  local copies, waits for them, and re-layouts  8.13 us (9%)
  matrix products  4.03 us (4%)
  other arithmetic  1.87 us (2%)
    all_to_all x1, starting transfers between devices, gram_rows(): lax.all_to_all(pieces, 'band', split_axis=2, concat_axis=1, tiled=True)  18.1 us
    all_to_all x1, waiting for transfers between devices, local(): piece = lax.all_to_all(slab, 'pw', split_axis=3, concat_axis=1, tiled=True)  14.4 us
    all_to_all x1, waiting for transfers between devices, local(): lax.all_to_all(payload, 'pw', split_axis=0, concat_axis=0, tiled=True)  13.3 us
    all_to_all x1, starting transfers between devices, local(): piece = lax.all_to_all(slab, 'pw', split_axis=3, concat_axis=1, tiled=True)  12.1 us
    all_to_all x1, waiting for transfers between devices, scatter_rows(): lax.all_to_all(partial, 'band', split_axis=2, concat_axis=0, tiled=True)  6.57 us
    all_to_all x1, starting transfers between devices, local(): lax.all_to_all(payload, 'pw', split_axis=0, concat_axis=0, tiled=True)  4.73 us
    all_to_all x1, starting transfers between devices, scatter_rows(): lax.all_to_all(partial, 'band', split_axis=2, concat_axis=0, tiled=True)  4.62 us
    all_to_all x1, waiting for transfers between devices, gram_rows(): lax.all_to_all(pieces, 'band', split_axis=2, concat_axis=1, tiled=True)  4.05 us
  transfers between devices with their start and end apart: 4, of which 4 were waited for; matrix products, arithmetic and copies ran while one was open for 7% of the time, Pallas kernels for 0%

profile of v11, /device:TPU:16, one launch (start us, length us, event | category | flops | bytes accessed | tf_op | source)
XLA Modules:
  0.0 92.9 jit_solution(16583493931048900965)
XLA Ops:
  0.6 0.8 reduce.6
  1.6 0.6 copy.100
  2.2 18.1 %all-to-all-start.1 = ((f32[2,1,32,108]{3,0,1,2:T(2,128)}), f32[2,1,32,108]{3,0,1,2:T(2,128)S(1)}, u32[]{:S(2)}, u32[]{:S(2)}) async-start(f32[2,1,32,108]{3,0,1,2:T(2,128)} %copy.100), calls=%async_computation.1 | async-start | bytes 65536 | tf_op jit(solution)/shard_map/all_to_all | solution.py:36
  20.4 0.3 reshape.122
  20.7 0.7 multiply_subtract_fusion
  21.4 0.2 eq.19
  22.0 0.7 fusion.4
  22.9 0.7 fusion.5
  23.6 0.9 %copy.97 = f32[1,3,2,96,96]{4,2,1,0,3:T(2,128)} copy(f32[1,3,2,96,96]{4,3,2,1,0:T(8,128)S(1)} %bitcast.88) | data formatting | bytes 442368 | tf_op jit(solution)/shard_map/reshape | solution.py:73
  24.8 4.0 %all-to-all-done.1 = f32[2,1,32,108]{3,0,1,2:T(2,128)S(1)} async-done(((f32[2,1,32,108]{3,0,1,2:T(2,128)}), f32[2,1,32,108]{3,0,1,2:T(2,128)S(1)}, u32[]{:S(2)}, u32[]{:S(2)}) %all-to-all-start.1) | async-done | bytes 27680 | tf_op jit(solution)/shard_map/all_to_all | solution.py:36
  28.8 12.1 %all-to-all-start = ((f32[1,3,2,96,96]{4,2,1,0,3:T(2,128)}), f32[1,3,2,96,96]{4,2,1,0,3:T(2,128)S(1)}, u32[]{:S(2)}, u32[]{:S(2)}) async-start(f32[1,3,2,96,96]{4,2,1,0,3:T(2,128)} %copy.97), calls=%async_computation | async-start | bytes 589824 | tf_op jit(solution)/shard_map/all_to_all | solution.py:74
  40.9 0.2 fusion.10
  41.2 14.4 %all-to-all-done = f32[1,3,2,96,96]{4,2,1,0,3:T(2,128)S(1)} async-done(((f32[1,3,2,96,96]{4,2,1,0,3:T(2,128)}), f32[1,3,2,96,96]{4,2,1,0,3:T(2,128)S(1)}, u32[]{:S(2)}, u32[]{:S(2)}) %all-to-all-start) | async-done | bytes 221216 | tf_op jit(solution)/shard_map/all_to_all | solution.py:74
  55.9 0.6 copy.107
  56.6 4.6 %all-to-all-start.2 = ((f32[1,2,32,1,32]{4,1,3,0,2:T(2,128)}), f32[1,2,32,1,32]{4,1,3,0,2:T(2,128)S(1)}, u32[]{:S(2)}, u32[]{:S(2)}) async-start(f32[1,2,32,1,32]{4,1,3,0,2:T(2,128)} %copy.107), calls=%async_computation.2 | async-start | bytes 65536 | tf_op jit(solution)/shard_map/all_to_all | solution.py:47
  61.2 0.5 convolution_multiply_fusion
  61.7 0.2 copy.104
  61.9 0.7 fusion.6
  62.6 0.2 copy.106
  62.8 0.2 transpose.33
  63.0 6.6 %all-to-all-done.2 = f32[1,2,32,1,32]{4,1,3,0,2:T(2,128)S(1)} async-done(((f32[1,2,32,1,32]{4,1,3,0,2:T(2,128)}), f32[1,2,32,1,32]{4,1,3,0,2:T(2,128)S(1)}, u32[]{:S(2)}, u32[]{:S(2)}) %all-to-all-start.2) | async-done | bytes 8224 | tf_op jit(solution)/shard_map/all_to_all | solution.py:47
  69.8 0.3 dynamic_update_slice.4
  70.1 0.9 copy.108
  71.0 4.7 %all-to-all-start.3 = ((f32[32,1,1792]{2,1,0:T(1,128)}), f32[32,1,1792]{2,1,0:T(1,128)S(1)}, u32[]{:S(2)}, u32[]{:S(2)}) async-start(f32[32,1,1792]{2,1,0:T(1,128)} %copy.108), calls=%async_computation.3 | async-start | bytes 458752 | tf_op jit(solution)/shard_map/all_to_all | solution.py:90
  75.8 13.3 %all-to-all-done.3 = f32[32,1,1792]{2,1,0:T(1,128)S(1)} async-done(((f32[32,1,1792]{2,1,0:T(1,128)}), f32[32,1,1792]{2,1,0:T(1,128)S(1)}, u32[]{:S(2)}, u32[]{:S(2)}) %all-to-all-start.3) | async-done | bytes 229408 | tf_op jit(solution)/shard_map/all_to_all | solution.py:90
  89.3 0.6 div.10
  89.9 0.3 reshape.130
  90.3 0.1 reshape.131
  90.4 0.7 convolution_bitcast_fusion
  91.2 0.6 fusion
  91.9 0.1 copy.113
  92.0 0.9 reshape.143
  (30 shorter events, 1.8 us)
Async XLA Ops:
  2.2 19.8 %copy-start = (f32[6,192,192]{2,1,0:T(8,128)S(1)}, f32[6,192,192]{2,1,0:T(8,128)}, u32[]{:S(2)}) copy-start(f32[6,192,192]{2,1,0:T(8,128)} %constant.15.clone) | copy-start | bytes 2654212
  2.2 26.6 %all-to-all-start.1 = ((f32[2,1,32,108]{3,0,1,2:T(2,128)}), f32[2,1,32,108]{3,0,1,2:T(2,128)S(1)}, u32[]{:S(2)}, u32[]{:S(2)}) async-start(f32[2,1,32,108]{3,0,1,2:T(2,128)} %copy.100), calls=%async_computation.1 | async-start | bytes 65536 | tf_op jit(solution)/shard_map/all_to_all | solution.py:36
  28.8 26.8 %all-to-all-start = ((f32[1,3,2,96,96]{4,2,1,0,3:T(2,128)}), f32[1,3,2,96,96]{4,2,1,0,3:T(2,128)S(1)}, u32[]{:S(2)}, u32[]{:S(2)}) async-start(f32[1,3,2,96,96]{4,2,1,0,3:T(2,128)} %copy.97), calls=%async_computation | async-start | bytes 589824 | tf_op jit(solution)/shard_map/all_to_all | solution.py:74
  40.9 20.3 %copy-start.1 = (f32[96,3,96]{2,0,1:T(8,128)S(1)}, f32[96,3,96]{2,0,1:T(8,128)}, u32[]{:S(2)}) copy-start(f32[96,3,96]{2,0,1:T(8,128)} %param.6) | copy-start | bytes 331780
  56.6 13.1 %all-to-all-start.2 = ((f32[1,2,32,1,32]{4,1,3,0,2:T(2,128)}), f32[1,2,32,1,32]{4,1,3,0,2:T(2,128)S(1)}, u32[]{:S(2)}, u32[]{:S(2)}) async-start(f32[1,2,32,1,32]{4,1,3,0,2:T(2,128)} %copy.107), calls=%async_computation.2 | async-start | bytes 65536 | tf_op jit(solution)/shard_map/all_to_all | solution.py:47
  71.0 18.2 %all-to-all-start.3 = ((f32[32,1,1792]{2,1,0:T(1,128)}), f32[32,1,1792]{2,1,0:T(1,128)S(1)}, u32[]{:S(2)}, u32[]{:S(2)}) async-start(f32[32,1,1792]{2,1,0:T(1,128)} %copy.108), calls=%async_computation.3 | async-start | bytes 458752 | tf_op jit(solution)/shard_map/all_to_all | solution.py:90
